TPU v7x, 256 devices: a whole 4x4x8 slice. The times are simulated.
256 devices in a mesh: seq: 32 (over z_lo, y, core), head: 8 (over x, z_hi).
Axes of the slice: x: 4, y: 4, z: 8 (z_hi: 2, z_lo: 4; z = z_hi * 4 + z_lo), core: 2. Of those that a mesh axis runs over, the one named last changes fastest.
Arguments:
- queries: bfloat16 [16384, 1024], P('seq', 'head'), may hold values from -2.5 to 2.5
- keys: bfloat16 [16384, 1024], P('seq', 'head'), may hold values from -2.5 to 2.5
- values: bfloat16 [16384, 1024], P('seq', 'head'), may hold values from -6 to 6
- attn_out: bfloat16 [16384, 1024], P('seq', 'head'), may hold values from -6 to 6
- out_grad: bfloat16 [16384, 1024], P('seq', 'head'), may hold values from -6 to 6
- lse: float32 [8, 16384], P('head', 'seq'), may hold values from 3.5 to 5.5
- trace_id: int32 [16384], replicated, may hold values from 0 to 127, never falling along the last dimension, each value on 1 to 384 neighbouring positions
- key_tiles: int32 [128, 48], P('seq'), may hold values from 0 to 127, as said below
- tile_count: int32 [128], P('seq'), may hold values from 1 to 48, as said below
- w_query: bfloat16 [1024, 1024], P(None, 'head'), may hold values from -0.1875 to 0.1875
- w_key: bfloat16 [1024, 1024], P(None, 'head'), may hold values from -0.1875 to 0.1875
- w_value: bfloat16 [1024, 1024], P(None, 'head'), may hold values from -0.1875 to 0.1875
- w_out: bfloat16 [1024, 1024], P('head'), may hold values from -0.1875 to 0.1875
Outputs:
- d_input: bfloat16 [16384, 1024], P('seq', 'head')
Inputs may be any that keep to these rules, and one draw needn't show every extreme that they name: `key_tiles`: each row lists 48 different key tiles and never its own tile; entries from position tile_count onward are not used. `tile_count`: some query tile uses all 48 entries. `trace_id`: trace numbers never fall along the tokens; one trace spans 384 tokens, none more.
All inputs are finite; a program needn't handle non-finite values.
Results may differ from a plain program's by a relative error of at most 0.015.
Values may be sent and summed in bfloat16 or wider, within the bound.
No kernel may reach another device: no remote copies, remote signals or barrier semaphores. Data moves between devices by JAX's collectives and lax.ppermute only.
A program may use at most 64 MiB of HBM per device.

v0:
```python
import jax
import jax.numpy as jnp
from jax import lax
from jax.sharding import PartitionSpec as P

HD = 128
TILE = 128
SEL = 48


def from_behind(value, axis, by):
    count = lax.axis_size(axis)
    return lax.ppermute(value, axis, [(i, (i + by) % count) for i in range(count)])


def pair_grads(query_heads, key_heads, value_heads, grad_heads, norm_rows, delta_rows, admit):
    scale = query_heads.shape[-1] ** (-0.5)
    scores = (
        jnp.einsum("rhd,chd->hrc", query_heads, key_heads, preferred_element_type=jnp.float32)
        * scale
    )
    probs = jnp.where(admit[None], jnp.exp(scores - norm_rows[:, :, None]), 0.0)
    value_grad = jnp.einsum(
        "hrc,rhd->chd", probs.astype(jnp.bfloat16), grad_heads, preferred_element_type=jnp.float32
    )
    prob_grad = jnp.einsum(
        "rhd,chd->hrc", grad_heads, value_heads, preferred_element_type=jnp.float32
    )
    score_grad = (probs * (prob_grad - delta_rows[:, :, None]) * scale).astype(jnp.bfloat16)
    query_grad = jnp.einsum(
        "hrc,chd->rhd", score_grad, key_heads, preferred_element_type=jnp.float32
    )
    key_grad = jnp.einsum(
        "hrc,rhd->chd", score_grad, query_heads, preferred_element_type=jnp.float32
    )
    return (query_grad, key_grad, value_grad)


def settle(total):
    part = lax.optimization_barrier(total.astype(jnp.bfloat16))
    return part.astype(jnp.float32)


def per_device(
    queries,
    keys,
    values,
    attn_out,
    out_grad,
    lse,
    trace_id,
    key_tiles,
    tile_count,
    w_query,
    w_key,
    w_value,
    w_out,
):
    tokens_here, width = queries.shape
    heads_here = width // HD
    seq_count = lax.axis_size("seq")
    seq_index = lax.axis_index("seq")
    tiles_here = tokens_here // TILE
    d_attn = lax.dot_general(
        lax.all_gather(out_grad, "head", axis=1, tiled=True),
        w_out,
        (((1,), (1,)), ((), ())),
        preferred_element_type=jnp.float32,
    ).astype(jnp.bfloat16)
    product = d_attn.astype(jnp.float32) * attn_out.astype(jnp.float32)
    delta = jnp.sum(product.reshape(tokens_here, heads_here, HD), axis=2).T
    query_heads = queries.reshape(tokens_here, heads_here, HD)
    key_heads = keys.reshape(tokens_here, heads_here, HD)
    value_heads = values.reshape(tokens_here, heads_here, HD)
    grad_heads = d_attn.reshape(tokens_here, heads_here, HD)
    trace_here = lax.dynamic_slice_in_dim(trace_id, seq_index * tokens_here, tokens_here, 0)
    slots = jnp.arange(SEL)[None, :] < tile_count[:, None]
    tile_range = jnp.arange(seq_count * tiles_here)
    allowed = jnp.any(
        (key_tiles[:, :, None] == tile_range[None, None, :]) & slots[:, :, None], axis=1
    )

    def visit(key_block, value_block, first_tile):
        block_tiles = key_block.shape[0] // TILE
        listed = lax.dynamic_slice(allowed, (0, first_tile), (tiles_here, block_tiles))
        trace_keys = lax.dynamic_slice_in_dim(trace_id, first_tile * TILE, key_block.shape[0], 0)
        admit = jnp.repeat(jnp.repeat(listed, TILE, axis=0), TILE, axis=1) & (
            trace_here[:, None] != trace_keys[None, :]
        )
        return pair_grads(query_heads, key_block, value_block, grad_heads, lse, delta, admit)

    zero_rows = jnp.zeros((tokens_here, heads_here, HD), jnp.float32)

    def pass_sums(sums):
        return from_behind(sums, "seq", 1)

    def cycle_work(step, held, sums, query_sum):
        source = (seq_index - step) % seq_count
        query_add, key_add, value_add = visit(held[0], held[1], source * tiles_here)
        return (query_sum + query_add, sums + jnp.stack([settle(key_add), settle(value_add)]))

    def cycle_turn(step, carry):
        held, sums, query_sum = carry
        query_sum, sums = cycle_work(step, held, sums, query_sum)
        held = from_behind(held, "seq", 1)
        return (held, pass_sums(sums), query_sum)

    start_carry = (
        jnp.stack([key_heads, value_heads]),
        jnp.stack([zero_rows, zero_rows]),
        zero_rows,
    )
    held, sums, query_sum = lax.fori_loop(0, seq_count - 1, cycle_turn, start_carry)
    query_sum, sums = cycle_work(seq_count - 1, held, sums, query_sum)
    sums = pass_sums(sums)
    key_sum, value_sum = (sums[0], sums[1])
    d_query = query_sum.astype(jnp.bfloat16).reshape(tokens_here, width)
    d_key = key_sum.astype(jnp.bfloat16).reshape(tokens_here, width)
    d_value = value_sum.astype(jnp.bfloat16).reshape(tokens_here, width)
    contract = (((1,), (1,)), ((), ()))
    total = lax.dot_general(w_query, d_query, contract, preferred_element_type=jnp.float32)
    total = total + lax.dot_general(w_key, d_key, contract, preferred_element_type=jnp.float32)
    d_input = lax.psum_scatter(
        total + lax.dot_general(w_value, d_value, contract, preferred_element_type=jnp.float32),
        "head",
        scatter_dimension=0,
        tiled=True,
    )
    return d_input.T.astype(jnp.bfloat16)


def solution(mesh):
    in_specs = (
        P("seq", "head"),
        P("seq", "head"),
        P("seq", "head"),
        P("seq", "head"),
        P("seq", "head"),
        P("head", "seq"),
        P(),
        P("seq", None),
        P("seq"),
        P(None, "head"),
        P(None, "head"),
        P(None, "head"),
        P("head", None),
    )
    out_specs = P("seq", "head")
    return jax.shard_map(
        per_device, mesh=mesh, in_specs=in_specs, out_specs=out_specs, check_vma=False
    )
```

profile of v0, /device:TPU:8, one launch (start us, length us, event | category | flops | bytes accessed | tf_op | source)
XLA Modules:
  0.0 790.5 jit_solution(7173864981957476666)
XLA Ops:
  12.3 61.9 %all-gather.2.cloned.1.call-done = bf16[512,1024]{1,0:T(8,128)(2,1)} async-done(((bf16[512,128]{1,0:T(8,128)(2,1)}), bf16[512,1024]{1,0:T(8,128)(2,1)}) %all-gather.2.cloned.1.call-update) | async-done | bytes 1048592 | tf_op jit(solution)/shard_map/all_gather | solution.py:65
  74.2 1.8 multiply_reduce_fusion
  76.2 585.5 %while.20 = (s32[]{:T(128)}, bf16[2,512,1,128]{3,1,2,0:T(8,128)(2,1)S(1)}, f32[2,512,1,128]{3,1,2,0:T(8,128)S(1)}, f32[512,1,128]{2,0,1:T(8,128)S(1)}, s32[]{:T(...) while((s32[]{:T(128)}, ...), condition=%wide.region_3.4_spmd.clone, body=%wide.region_2.3_spmd.clone.sunk | while | flops 338821152 | bytes 11944476 | solution.py:113
  82.3 9.5 %collective-permute-done = bf16[2,512,1,128]{3,1,2,0:T(8,128)(2,1)S(1)} collective-permute-done((bf16[2,512,1,128]{3,1,2,0:T(8,128)(2,1)S(1)}, bf16[2,512,1,128]{3,1,2,0:T(8,128)(2,1)S(1)}, u32[]{:S(2)}, u32[]{:S(2)}) %collective-permute-start) | collective-permute-done | bytes 262176 | tf_op jit(solution)/shard_map/while/body/eval_jaxpr/ppermute | solution.py:13
  92.7 1.6 broadcast_in_dim.75
  97.9 9.5 %collective-permute-done = bf16[2,512,1,128]{3,1,2,0:T(8,128)(2,1)S(1)} collective-permute-done((bf16[2,512,1,128]{3,1,2,0:T(8,128)(2,1)S(1)}, bf16[2,512,1,128]{3,1,2,0:T(8,128)(2,1)S(1)}, u32[]{:S(2)}, u32[]{:S(2)}) %collective-permute-start) | collective-permute-done | bytes 262176 | tf_op jit(solution)/shard_map/while/body/eval_jaxpr/ppermute | solution.py:13
  108.3 1.6 broadcast_in_dim.75
  113.5 9.5 %collective-permute-done = bf16[2,512,1,128]{3,1,2,0:T(8,128)(2,1)S(1)} collective-permute-done((bf16[2,512,1,128]{3,1,2,0:T(8,128)(2,1)S(1)}, bf16[2,512,1,128]{3,1,2,0:T(8,128)(2,1)S(1)}, u32[]{:S(2)}, u32[]{:S(2)}) %collective-permute-start) | collective-permute-done | bytes 262176 | tf_op jit(solution)/shard_map/while/body/eval_jaxpr/ppermute | solution.py:13
  123.8 1.6 broadcast_in_dim.75
  129.0 9.5 %collective-permute-done = bf16[2,512,1,128]{3,1,2,0:T(8,128)(2,1)S(1)} collective-permute-done((bf16[2,512,1,128]{3,1,2,0:T(8,128)(2,1)S(1)}, bf16[2,512,1,128]{3,1,2,0:T(8,128)(2,1)S(1)}, u32[]{:S(2)}, u32[]{:S(2)}) %collective-permute-start) | collective-permute-done | bytes 262176 | tf_op jit(solution)/shard_map/while/body/eval_jaxpr/ppermute | solution.py:13
  144.6 10.5 %collective-permute-done = bf16[2,512,1,128]{3,1,2,0:T(8,128)(2,1)S(1)} collective-permute-done((bf16[2,512,1,128]{3,1,2,0:T(8,128)(2,1)S(1)}, bf16[2,512,1,128]{3,1,2,0:T(8,128)(2,1)S(1)}, u32[]{:S(2)}, u32[]{:S(2)}) %collective-permute-start) | collective-permute-done | bytes 262176 | tf_op jit(solution)/shard_map/while/body/eval_jaxpr/ppermute | solution.py:13
  156.0 1.6 broadcast_in_dim.75
  160.2 14.4 %collective-permute-done = bf16[2,512,1,128]{3,1,2,0:T(8,128)(2,1)S(1)} collective-permute-done((bf16[2,512,1,128]{3,1,2,0:T(8,128)(2,1)S(1)}, bf16[2,512,1,128]{3,1,2,0:T(8,128)(2,1)S(1)}, u32[]{:S(2)}, u32[]{:S(2)}) %collective-permute-start) | collective-permute-done | bytes 262176 | tf_op jit(solution)/shard_map/while/body/eval_jaxpr/ppermute | solution.py:13
  179.2 14.9 %collective-permute-done = bf16[2,512,1,128]{3,1,2,0:T(8,128)(2,1)S(1)} collective-permute-done((bf16[2,512,1,128]{3,1,2,0:T(8,128)(2,1)S(1)}, bf16[2,512,1,128]{3,1,2,0:T(8,128)(2,1)S(1)}, u32[]{:S(2)}, u32[]{:S(2)}) %collective-permute-start) | collective-permute-done | bytes 262176 | tf_op jit(solution)/shard_map/while/body/eval_jaxpr/ppermute | solution.py:13
  195.0 1.6 broadcast_in_dim.75
  198.7 14.9 %collective-permute-done = bf16[2,512,1,128]{3,1,2,0:T(8,128)(2,1)S(1)} collective-permute-done((bf16[2,512,1,128]{3,1,2,0:T(8,128)(2,1)S(1)}, bf16[2,512,1,128]{3,1,2,0:T(8,128)(2,1)S(1)}, u32[]{:S(2)}, u32[]{:S(2)}) %collective-permute-start) | collective-permute-done | bytes 262176 | tf_op jit(solution)/shard_map/while/body/eval_jaxpr/ppermute | solution.py:13
  214.4 1.6 broadcast_in_dim.75
  218.1 14.9 %collective-permute-done = bf16[2,512,1,128]{3,1,2,0:T(8,128)(2,1)S(1)} collective-permute-done((bf16[2,512,1,128]{3,1,2,0:T(8,128)(2,1)S(1)}, bf16[2,512,1,128]{3,1,2,0:T(8,128)(2,1)S(1)}, u32[]{:S(2)}, u32[]{:S(2)}) %collective-permute-start) | collective-permute-done | bytes 262176 | tf_op jit(solution)/shard_map/while/body/eval_jaxpr/ppermute | solution.py:13
  237.6 14.9 %collective-permute-done = bf16[2,512,1,128]{3,1,2,0:T(8,128)(2,1)S(1)} collective-permute-done((bf16[2,512,1,128]{3,1,2,0:T(8,128)(2,1)S(1)}, bf16[2,512,1,128]{3,1,2,0:T(8,128)(2,1)S(1)}, u32[]{:S(2)}, u32[]{:S(2)}) %collective-permute-start) | collective-permute-done | bytes 262176 | tf_op jit(solution)/shard_map/while/body/eval_jaxpr/ppermute | solution.py:13
  253.4 1.6 broadcast_in_dim.75
  257.1 14.9 %collective-permute-done = bf16[2,512,1,128]{3,1,2,0:T(8,128)(2,1)S(1)} collective-permute-done((bf16[2,512,1,128]{3,1,2,0:T(8,128)(2,1)S(1)}, bf16[2,512,1,128]{3,1,2,0:T(8,128)(2,1)S(1)}, u32[]{:S(2)}, u32[]{:S(2)}) %collective-permute-start) | collective-permute-done | bytes 262176 | tf_op jit(solution)/shard_map/while/body/eval_jaxpr/ppermute | solution.py:13
  272.9 1.6 broadcast_in_dim.75
  276.6 14.9 %collective-permute-done = bf16[2,512,1,128]{3,1,2,0:T(8,128)(2,1)S(1)} collective-permute-done((bf16[2,512,1,128]{3,1,2,0:T(8,128)(2,1)S(1)}, bf16[2,512,1,128]{3,1,2,0:T(8,128)(2,1)S(1)}, u32[]{:S(2)}, u32[]{:S(2)}) %collective-permute-start) | collective-permute-done | bytes 262176 | tf_op jit(solution)/shard_map/while/body/eval_jaxpr/ppermute | solution.py:13
  292.4 1.6 broadcast_in_dim.75
  296.1 14.9 %collective-permute-done = bf16[2,512,1,128]{3,1,2,0:T(8,128)(2,1)S(1)} collective-permute-done((bf16[2,512,1,128]{3,1,2,0:T(8,128)(2,1)S(1)}, bf16[2,512,1,128]{3,1,2,0:T(8,128)(2,1)S(1)}, u32[]{:S(2)}, u32[]{:S(2)}) %collective-permute-start) | collective-permute-done | bytes 262176 | tf_op jit(solution)/shard_map/while/body/eval_jaxpr/ppermute | solution.py:13
  315.5 14.9 %collective-permute-done = bf16[2,512,1,128]{3,1,2,0:T(8,128)(2,1)S(1)} collective-permute-done((bf16[2,512,1,128]{3,1,2,0:T(8,128)(2,1)S(1)}, bf16[2,512,1,128]{3,1,2,0:T(8,128)(2,1)S(1)}, u32[]{:S(2)}, u32[]{:S(2)}) %collective-permute-start) | collective-permute-done | bytes 262176 | tf_op jit(solution)/shard_map/while/body/eval_jaxpr/ppermute | solution.py:13
  335.0 14.9 %collective-permute-done = bf16[2,512,1,128]{3,1,2,0:T(8,128)(2,1)S(1)} collective-permute-done((bf16[2,512,1,128]{3,1,2,0:T(8,128)(2,1)S(1)}, bf16[2,512,1,128]{3,1,2,0:T(8,128)(2,1)S(1)}, u32[]{:S(2)}, u32[]{:S(2)}) %collective-permute-start) | collective-permute-done | bytes 262176 | tf_op jit(solution)/shard_map/while/body/eval_jaxpr/ppermute | solution.py:13
  354.5 14.9 %collective-permute-done = bf16[2,512,1,128]{3,1,2,0:T(8,128)(2,1)S(1)} collective-permute-done((bf16[2,512,1,128]{3,1,2,0:T(8,128)(2,1)S(1)}, bf16[2,512,1,128]{3,1,2,0:T(8,128)(2,1)S(1)}, u32[]{:S(2)}, u32[]{:S(2)}) %collective-permute-start) | collective-permute-done | bytes 262176 | tf_op jit(solution)/shard_map/while/body/eval_jaxpr/ppermute | solution.py:13
  374.0 14.9 %collective-permute-done = bf16[2,512,1,128]{3,1,2,0:T(8,128)(2,1)S(1)} collective-permute-done((bf16[2,512,1,128]{3,1,2,0:T(8,128)(2,1)S(1)}, bf16[2,512,1,128]{3,1,2,0:T(8,128)(2,1)S(1)}, u32[]{:S(2)}, u32[]{:S(2)}) %collective-permute-start) | collective-permute-done | bytes 262176 | tf_op jit(solution)/shard_map/while/body/eval_jaxpr/ppermute | solution.py:13
  393.5 14.9 %collective-permute-done = bf16[2,512,1,128]{3,1,2,0:T(8,128)(2,1)S(1)} collective-permute-done((bf16[2,512,1,128]{3,1,2,0:T(8,128)(2,1)S(1)}, bf16[2,512,1,128]{3,1,2,0:T(8,128)(2,1)S(1)}, u32[]{:S(2)}, u32[]{:S(2)}) %collective-permute-start) | collective-permute-done | bytes 262176 | tf_op jit(solution)/shard_map/while/body/eval_jaxpr/ppermute | solution.py:13
  413.0 14.9 %collective-permute-done = bf16[2,512,1,128]{3,1,2,0:T(8,128)(2,1)S(1)} collective-permute-done((bf16[2,512,1,128]{3,1,2,0:T(8,128)(2,1)S(1)}, bf16[2,512,1,128]{3,1,2,0:T(8,128)(2,1)S(1)}, u32[]{:S(2)}, u32[]{:S(2)}) %collective-permute-start) | collective-permute-done | bytes 262176 | tf_op jit(solution)/shard_map/while/body/eval_jaxpr/ppermute | solution.py:13
  432.4 14.9 %collective-permute-done = bf16[2,512,1,128]{3,1,2,0:T(8,128)(2,1)S(1)} collective-permute-done((bf16[2,512,1,128]{3,1,2,0:T(8,128)(2,1)S(1)}, bf16[2,512,1,128]{3,1,2,0:T(8,128)(2,1)S(1)}, u32[]{:S(2)}, u32[]{:S(2)}) %collective-permute-start) | collective-permute-done | bytes 262176 | tf_op jit(solution)/shard_map/while/body/eval_jaxpr/ppermute | solution.py:13
  451.9 14.9 %collective-permute-done = bf16[2,512,1,128]{3,1,2,0:T(8,128)(2,1)S(1)} collective-permute-done((bf16[2,512,1,128]{3,1,2,0:T(8,128)(2,1)S(1)}, bf16[2,512,1,128]{3,1,2,0:T(8,128)(2,1)S(1)}, u32[]{:S(2)}, u32[]{:S(2)}) %collective-permute-start) | collective-permute-done | bytes 262176 | tf_op jit(solution)/shard_map/while/body/eval_jaxpr/ppermute | solution.py:13
  471.4 14.9 %collective-permute-done = bf16[2,512,1,128]{3,1,2,0:T(8,128)(2,1)S(1)} collective-permute-done((bf16[2,512,1,128]{3,1,2,0:T(8,128)(2,1)S(1)}, bf16[2,512,1,128]{3,1,2,0:T(8,128)(2,1)S(1)}, u32[]{:S(2)}, u32[]{:S(2)}) %collective-permute-start) | collective-permute-done | bytes 262176 | tf_op jit(solution)/shard_map/while/body/eval_jaxpr/ppermute | solution.py:13
  490.9 14.9 %collective-permute-done = bf16[2,512,1,128]{3,1,2,0:T(8,128)(2,1)S(1)} collective-permute-done((bf16[2,512,1,128]{3,1,2,0:T(8,128)(2,1)S(1)}, bf16[2,512,1,128]{3,1,2,0:T(8,128)(2,1)S(1)}, u32[]{:S(2)}, u32[]{:S(2)}) %collective-permute-start) | collective-permute-done | bytes 262176 | tf_op jit(solution)/shard_map/while/body/eval_jaxpr/ppermute | solution.py:13
  510.4 14.9 %collective-permute-done = bf16[2,512,1,128]{3,1,2,0:T(8,128)(2,1)S(1)} collective-permute-done((bf16[2,512,1,128]{3,1,2,0:T(8,128)(2,1)S(1)}, bf16[2,512,1,128]{3,1,2,0:T(8,128)(2,1)S(1)}, u32[]{:S(2)}, u32[]{:S(2)}) %collective-permute-start) | collective-permute-done | bytes 262176 | tf_op jit(solution)/shard_map/while/body/eval_jaxpr/ppermute | solution.py:13
  529.9 14.9 %collective-permute-done = bf16[2,512,1,128]{3,1,2,0:T(8,128)(2,1)S(1)} collective-permute-done((bf16[2,512,1,128]{3,1,2,0:T(8,128)(2,1)S(1)}, bf16[2,512,1,128]{3,1,2,0:T(8,128)(2,1)S(1)}, u32[]{:S(2)}, u32[]{:S(2)}) %collective-permute-start) | collective-permute-done | bytes 262176 | tf_op jit(solution)/shard_map/while/body/eval_jaxpr/ppermute | solution.py:13
  549.3 14.9 %collective-permute-done = bf16[2,512,1,128]{3,1,2,0:T(8,128)(2,1)S(1)} collective-permute-done((bf16[2,512,1,128]{3,1,2,0:T(8,128)(2,1)S(1)}, bf16[2,512,1,128]{3,1,2,0:T(8,128)(2,1)S(1)}, u32[]{:S(2)}, u32[]{:S(2)}) %collective-permute-start) | collective-permute-done | bytes 262176 | tf_op jit(solution)/shard_map/while/body/eval_jaxpr/ppermute | solution.py:13
  568.8 14.9 %collective-permute-done = bf16[2,512,1,128]{3,1,2,0:T(8,128)(2,1)S(1)} collective-permute-done((bf16[2,512,1,128]{3,1,2,0:T(8,128)(2,1)S(1)}, bf16[2,512,1,128]{3,1,2,0:T(8,128)(2,1)S(1)}, u32[]{:S(2)}, u32[]{:S(2)}) %collective-permute-start) | collective-permute-done | bytes 262176 | tf_op jit(solution)/shard_map/while/body/eval_jaxpr/ppermute | solution.py:13
  588.3 14.9 %collective-permute-done = bf16[2,512,1,128]{3,1,2,0:T(8,128)(2,1)S(1)} collective-permute-done((bf16[2,512,1,128]{3,1,2,0:T(8,128)(2,1)S(1)}, bf16[2,512,1,128]{3,1,2,0:T(8,128)(2,1)S(1)}, u32[]{:S(2)}, u32[]{:S(2)}) %collective-permute-start) | collective-permute-done | bytes 262176 | tf_op jit(solution)/shard_map/while/body/eval_jaxpr/ppermute | solution.py:13
  607.8 14.9 %collective-permute-done = bf16[2,512,1,128]{3,1,2,0:T(8,128)(2,1)S(1)} collective-permute-done((bf16[2,512,1,128]{3,1,2,0:T(8,128)(2,1)S(1)}, bf16[2,512,1,128]{3,1,2,0:T(8,128)(2,1)S(1)}, u32[]{:S(2)}, u32[]{:S(2)}) %collective-permute-start) | collective-permute-done | bytes 262176 | tf_op jit(solution)/shard_map/while/body/eval_jaxpr/ppermute | solution.py:13
  627.3 14.9 %collective-permute-done = bf16[2,512,1,128]{3,1,2,0:T(8,128)(2,1)S(1)} collective-permute-done((bf16[2,512,1,128]{3,1,2,0:T(8,128)(2,1)S(1)}, bf16[2,512,1,128]{3,1,2,0:T(8,128)(2,1)S(1)}, u32[]{:S(2)}, u32[]{:S(2)}) %collective-permute-start) | collective-permute-done | bytes 262176 | tf_op jit(solution)/shard_map/while/body/eval_jaxpr/ppermute | solution.py:13
  646.7 14.9 %collective-permute-done = bf16[2,512,1,128]{3,1,2,0:T(8,128)(2,1)S(1)} collective-permute-done((bf16[2,512,1,128]{3,1,2,0:T(8,128)(2,1)S(1)}, bf16[2,512,1,128]{3,1,2,0:T(8,128)(2,1)S(1)}, u32[]{:S(2)}, u32[]{:S(2)}) %collective-permute-start) | collective-permute-done | bytes 262176 | tf_op jit(solution)/shard_map/while/body/eval_jaxpr/ppermute | solution.py:13
  663.3 2.0 fusion.32
  665.3 7.6 collective-permute-done.2
  673.4 1.8 add_bitcast_fusion
  675.2 106.9 %reduce-scatter.2.cloned.1.call-done = f32[128,512]{0,1:T(8,128)} async-done(((f32[1024,512]{0,1:T(8,128)}), f32[128,512]{0,1:T(8,128)}) %reduce-scatter.2.cloned.1.call-update) | async-done | bytes 262160 | tf_op jit(solution)/shard_map/reduce_scatter | solution.py:123
  782.0 1.6 convert_bitcast_fusion
  (462 shorter events, 141.4 us)
Async XLA Ops:
  6.5 67.7 %all-gather.2.cloned.1.call-start = ((), (), s32[]{:S(2)}) async-start(), calls=%async_computation.1 | async-start | bytes 1179648 | tf_op jit(solution)/shard_map/all_gather | solution.py:65
  7.3 774.8 %reduce-scatter.2.cloned.1.call-start = ((), (), s32[]{:S(2)}) async-start(), calls=%async_computation.2 | async-start | bytes 2359296 | tf_op jit(solution)/shard_map/reduce_scatter | solution.py:123
  159.2 15.4 %collective-permute-start.1 = (f32[2,512,1,128]{3,1,2,0:T(8,128)S(1)}, f32[2,512,1,128]{3,1,2,0:T(8,128)S(1)}, u32[]{:S(2)}, u32[]{:S(2)}) collective-permute-start(f32[2,512,1,128]{3,1,2,0:T(8,128)S(1)} %convert_add_fusion.3), channel_id=1, source_target_pairs={{0,8},{8,16},{16,24},{24,32},{32,40},{40,48},{48,56},{56,64},{64,7... | collective-permute-start | bytes 1572872 | tf_op jit(solution)/shard_map/while/body/eval_jaxpr/ppermute | solution.py:13
  159.3 15.3 %collective-permute-start = (bf16[2,512,1,128]{3,1,2,0:T(8,128)(2,1)S(1)}, bf16[2,512,1,128]{3,1,2,0:T(8,128)(2,1)S(1)}, u32[]{:S(2)}, u32[]{:S(2)}) collective-permute-start(bf16[2,512,1,128]{3,1,2,0:T(8,128)(2,1)S(1)} %copy.49), channel_id=1, source_target_pairs={{0,8},{8,16},{16,24},{24,32},{32,40},{40,48},{48,56},{56,64},{64,7... | collective-permute-start | bytes 786440 | tf_op jit(solution)/shard_map/while/body/eval_jaxpr/ppermute | solution.py:13
  178.7 15.4 %collective-permute-start.1 = (f32[2,512,1,128]{3,1,2,0:T(8,128)S(1)}, f32[2,512,1,128]{3,1,2,0:T(8,128)S(1)}, u32[]{:S(2)}, u32[]{:S(2)}) collective-permute-start(f32[2,512,1,128]{3,1,2,0:T(8,128)S(1)} %convert_add_fusion.3), channel_id=1, source_target_pairs={{0,8},{8,16},{16,24},{24,32},{32,40},{40,48},{48,56},{56,64},{64,7... | collective-permute-start | bytes 1572872 | tf_op jit(solution)/shard_map/while/body/eval_jaxpr/ppermute | solution.py:13
  178.7 15.3 %collective-permute-start = (bf16[2,512,1,128]{3,1,2,0:T(8,128)(2,1)S(1)}, bf16[2,512,1,128]{3,1,2,0:T(8,128)(2,1)S(1)}, u32[]{:S(2)}, u32[]{:S(2)}) collective-permute-start(bf16[2,512,1,128]{3,1,2,0:T(8,128)(2,1)S(1)} %copy.49), channel_id=1, source_target_pairs={{0,8},{8,16},{16,24},{24,32},{32,40},{40,48},{48,56},{56,64},{64,7... | collective-permute-start | bytes 786440 | tf_op jit(solution)/shard_map/while/body/eval_jaxpr/ppermute | solution.py:13
  198.1 15.4 %collective-permute-start.1 = (f32[2,512,1,128]{3,1,2,0:T(8,128)S(1)}, f32[2,512,1,128]{3,1,2,0:T(8,128)S(1)}, u32[]{:S(2)}, u32[]{:S(2)}) collective-permute-start(f32[2,512,1,128]{3,1,2,0:T(8,128)S(1)} %convert_add_fusion.3), channel_id=1, source_target_pairs={{0,8},{8,16},{16,24},{24,32},{32,40},{40,48},{48,56},{56,64},{64,7... | collective-permute-start | bytes 1572872 | tf_op jit(solution)/shard_map/while/body/eval_jaxpr/ppermute | solution.py:13
  198.2 15.3 %collective-permute-start = (bf16[2,512,1,128]{3,1,2,0:T(8,128)(2,1)S(1)}, bf16[2,512,1,128]{3,1,2,0:T(8,128)(2,1)S(1)}, u32[]{:S(2)}, u32[]{:S(2)}) collective-permute-start(bf16[2,512,1,128]{3,1,2,0:T(8,128)(2,1)S(1)} %copy.49), channel_id=1, source_target_pairs={{0,8},{8,16},{16,24},{24,32},{32,40},{40,48},{48,56},{56,64},{64,7... | collective-permute-start | bytes 786440 | tf_op jit(solution)/shard_map/while/body/eval_jaxpr/ppermute | solution.py:13
  217.6 15.4 %collective-permute-start.1 = (f32[2,512,1,128]{3,1,2,0:T(8,128)S(1)}, f32[2,512,1,128]{3,1,2,0:T(8,128)S(1)}, u32[]{:S(2)}, u32[]{:S(2)}) collective-permute-start(f32[2,512,1,128]{3,1,2,0:T(8,128)S(1)} %convert_add_fusion.3), channel_id=1, source_target_pairs={{0,8},{8,16},{16,24},{24,32},{32,40},{40,48},{48,56},{56,64},{64,7... | collective-permute-start | bytes 1572872 | tf_op jit(solution)/shard_map/while/body/eval_jaxpr/ppermute | solution.py:13
  217.7 15.3 %collective-permute-start = (bf16[2,512,1,128]{3,1,2,0:T(8,128)(2,1)S(1)}, bf16[2,512,1,128]{3,1,2,0:T(8,128)(2,1)S(1)}, u32[]{:S(2)}, u32[]{:S(2)}) collective-permute-start(bf16[2,512,1,128]{3,1,2,0:T(8,128)(2,1)S(1)} %copy.49), channel_id=1, source_target_pairs={{0,8},{8,16},{16,24},{24,32},{32,40},{40,48},{48,56},{56,64},{64,7... | collective-permute-start | bytes 786440 | tf_op jit(solution)/shard_map/while/body/eval_jaxpr/ppermute | solution.py:13
  237.1 15.4 %collective-permute-start.1 = (f32[2,512,1,128]{3,1,2,0:T(8,128)S(1)}, f32[2,512,1,128]{3,1,2,0:T(8,128)S(1)}, u32[]{:S(2)}, u32[]{:S(2)}) collective-permute-start(f32[2,512,1,128]{3,1,2,0:T(8,128)S(1)} %convert_add_fusion.3), channel_id=1, source_target_pairs={{0,8},{8,16},{16,24},{24,32},{32,40},{40,48},{48,56},{56,64},{64,7... | collective-permute-start | bytes 1572872 | tf_op jit(solution)/shard_map/while/body/eval_jaxpr/ppermute | solution.py:13
  237.2 15.3 %collective-permute-start = (bf16[2,512,1,128]{3,1,2,0:T(8,128)(2,1)S(1)}, bf16[2,512,1,128]{3,1,2,0:T(8,128)(2,1)S(1)}, u32[]{:S(2)}, u32[]{:S(2)}) collective-permute-start(bf16[2,512,1,128]{3,1,2,0:T(8,128)(2,1)S(1)} %copy.49), channel_id=1, source_target_pairs={{0,8},{8,16},{16,24},{24,32},{32,40},{40,48},{48,56},{56,64},{64,7... | collective-permute-start | bytes 786440 | tf_op jit(solution)/shard_map/while/body/eval_jaxpr/ppermute | solution.py:13
  256.6 15.4 %collective-permute-start.1 = (f32[2,512,1,128]{3,1,2,0:T(8,128)S(1)}, f32[2,512,1,128]{3,1,2,0:T(8,128)S(1)}, u32[]{:S(2)}, u32[]{:S(2)}) collective-permute-start(f32[2,512,1,128]{3,1,2,0:T(8,128)S(1)} %convert_add_fusion.3), channel_id=1, source_target_pairs={{0,8},{8,16},{16,24},{24,32},{32,40},{40,48},{48,56},{56,64},{64,7... | collective-permute-start | bytes 1572872 | tf_op jit(solution)/shard_map/while/body/eval_jaxpr/ppermute | solution.py:13
  256.7 15.3 %collective-permute-start = (bf16[2,512,1,128]{3,1,2,0:T(8,128)(2,1)S(1)}, bf16[2,512,1,128]{3,1,2,0:T(8,128)(2,1)S(1)}, u32[]{:S(2)}, u32[]{:S(2)}) collective-permute-start(bf16[2,512,1,128]{3,1,2,0:T(8,128)(2,1)S(1)} %copy.49), channel_id=1, source_target_pairs={{0,8},{8,16},{16,24},{24,32},{32,40},{40,48},{48,56},{56,64},{64,7... | collective-permute-start | bytes 786440 | tf_op jit(solution)/shard_map/while/body/eval_jaxpr/ppermute | solution.py:13
  276.1 15.4 %collective-permute-start.1 = (f32[2,512,1,128]{3,1,2,0:T(8,128)S(1)}, f32[2,512,1,128]{3,1,2,0:T(8,128)S(1)}, u32[]{:S(2)}, u32[]{:S(2)}) collective-permute-start(f32[2,512,1,128]{3,1,2,0:T(8,128)S(1)} %convert_add_fusion.3), channel_id=1, source_target_pairs={{0,8},{8,16},{16,24},{24,32},{32,40},{40,48},{48,56},{56,64},{64,7... | collective-permute-start | bytes 1572872 | tf_op jit(solution)/shard_map/while/body/eval_jaxpr/ppermute | solution.py:13
  276.2 15.3 %collective-permute-start = (bf16[2,512,1,128]{3,1,2,0:T(8,128)(2,1)S(1)}, bf16[2,512,1,128]{3,1,2,0:T(8,128)(2,1)S(1)}, u32[]{:S(2)}, u32[]{:S(2)}) collective-permute-start(bf16[2,512,1,128]{3,1,2,0:T(8,128)(2,1)S(1)} %copy.49), channel_id=1, source_target_pairs={{0,8},{8,16},{16,24},{24,32},{32,40},{40,48},{48,56},{56,64},{64,7... | collective-permute-start | bytes 786440 | tf_op jit(solution)/shard_map/while/body/eval_jaxpr/ppermute | solution.py:13
  295.5 15.4 %collective-permute-start.1 = (f32[2,512,1,128]{3,1,2,0:T(8,128)S(1)}, f32[2,512,1,128]{3,1,2,0:T(8,128)S(1)}, u32[]{:S(2)}, u32[]{:S(2)}) collective-permute-start(f32[2,512,1,128]{3,1,2,0:T(8,128)S(1)} %convert_add_fusion.3), channel_id=1, source_target_pairs={{0,8},{8,16},{16,24},{24,32},{32,40},{40,48},{48,56},{56,64},{64,7... | collective-permute-start | bytes 1572872 | tf_op jit(solution)/shard_map/while/body/eval_jaxpr/ppermute | solution.py:13
  295.6 15.3 %collective-permute-start = (bf16[2,512,1,128]{3,1,2,0:T(8,128)(2,1)S(1)}, bf16[2,512,1,128]{3,1,2,0:T(8,128)(2,1)S(1)}, u32[]{:S(2)}, u32[]{:S(2)}) collective-permute-start(bf16[2,512,1,128]{3,1,2,0:T(8,128)(2,1)S(1)} %copy.49), channel_id=1, source_target_pairs={{0,8},{8,16},{16,24},{24,32},{32,40},{40,48},{48,56},{56,64},{64,7... | collective-permute-start | bytes 786440 | tf_op jit(solution)/shard_map/while/body/eval_jaxpr/ppermute | solution.py:13
  315.0 15.4 %collective-permute-start.1 = (f32[2,512,1,128]{3,1,2,0:T(8,128)S(1)}, f32[2,512,1,128]{3,1,2,0:T(8,128)S(1)}, u32[]{:S(2)}, u32[]{:S(2)}) collective-permute-start(f32[2,512,1,128]{3,1,2,0:T(8,128)S(1)} %convert_add_fusion.3), channel_id=1, source_target_pairs={{0,8},{8,16},{16,24},{24,32},{32,40},{40,48},{48,56},{56,64},{64,7... | collective-permute-start | bytes 1572872 | tf_op jit(solution)/shard_map/while/body/eval_jaxpr/ppermute | solution.py:13
  315.1 15.3 %collective-permute-start = (bf16[2,512,1,128]{3,1,2,0:T(8,128)(2,1)S(1)}, bf16[2,512,1,128]{3,1,2,0:T(8,128)(2,1)S(1)}, u32[]{:S(2)}, u32[]{:S(2)}) collective-permute-start(bf16[2,512,1,128]{3,1,2,0:T(8,128)(2,1)S(1)} %copy.49), channel_id=1, source_target_pairs={{0,8},{8,16},{16,24},{24,32},{32,40},{40,48},{48,56},{56,64},{64,7... | collective-permute-start | bytes 786440 | tf_op jit(solution)/shard_map/while/body/eval_jaxpr/ppermute | solution.py:13
  334.5 15.4 %collective-permute-start.1 = (f32[2,512,1,128]{3,1,2,0:T(8,128)S(1)}, f32[2,512,1,128]{3,1,2,0:T(8,128)S(1)}, u32[]{:S(2)}, u32[]{:S(2)}) collective-permute-start(f32[2,512,1,128]{3,1,2,0:T(8,128)S(1)} %convert_add_fusion.3), channel_id=1, source_target_pairs={{0,8},{8,16},{16,24},{24,32},{32,40},{40,48},{48,56},{56,64},{64,7... | collective-permute-start | bytes 1572872 | tf_op jit(solution)/shard_map/while/body/eval_jaxpr/ppermute | solution.py:13
  334.6 15.3 %collective-permute-start = (bf16[2,512,1,128]{3,1,2,0:T(8,128)(2,1)S(1)}, bf16[2,512,1,128]{3,1,2,0:T(8,128)(2,1)S(1)}, u32[]{:S(2)}, u32[]{:S(2)}) collective-permute-start(bf16[2,512,1,128]{3,1,2,0:T(8,128)(2,1)S(1)} %copy.49), channel_id=1, source_target_pairs={{0,8},{8,16},{16,24},{24,32},{32,40},{40,48},{48,56},{56,64},{64,7... | collective-permute-start | bytes 786440 | tf_op jit(solution)/shard_map/while/body/eval_jaxpr/ppermute | solution.py:13
  354.0 15.4 %collective-permute-start.1 = (f32[2,512,1,128]{3,1,2,0:T(8,128)S(1)}, f32[2,512,1,128]{3,1,2,0:T(8,128)S(1)}, u32[]{:S(2)}, u32[]{:S(2)}) collective-permute-start(f32[2,512,1,128]{3,1,2,0:T(8,128)S(1)} %convert_add_fusion.3), channel_id=1, source_target_pairs={{0,8},{8,16},{16,24},{24,32},{32,40},{40,48},{48,56},{56,64},{64,7... | collective-permute-start | bytes 1572872 | tf_op jit(solution)/shard_map/while/body/eval_jaxpr/ppermute | solution.py:13
  354.1 15.3 %collective-permute-start = (bf16[2,512,1,128]{3,1,2,0:T(8,128)(2,1)S(1)}, bf16[2,512,1,128]{3,1,2,0:T(8,128)(2,1)S(1)}, u32[]{:S(2)}, u32[]{:S(2)}) collective-permute-start(bf16[2,512,1,128]{3,1,2,0:T(8,128)(2,1)S(1)} %copy.49), channel_id=1, source_target_pairs={{0,8},{8,16},{16,24},{24,32},{32,40},{40,48},{48,56},{56,64},{64,7... | collective-permute-start | bytes 786440 | tf_op jit(solution)/shard_map/while/body/eval_jaxpr/ppermute | solution.py:13
  373.5 15.4 %collective-permute-start.1 = (f32[2,512,1,128]{3,1,2,0:T(8,128)S(1)}, f32[2,512,1,128]{3,1,2,0:T(8,128)S(1)}, u32[]{:S(2)}, u32[]{:S(2)}) collective-permute-start(f32[2,512,1,128]{3,1,2,0:T(8,128)S(1)} %convert_add_fusion.3), channel_id=1, source_target_pairs={{0,8},{8,16},{16,24},{24,32},{32,40},{40,48},{48,56},{56,64},{64,7... | collective-permute-start | bytes 1572872 | tf_op jit(solution)/shard_map/while/body/eval_jaxpr/ppermute | solution.py:13
  373.6 15.3 %collective-permute-start = (bf16[2,512,1,128]{3,1,2,0:T(8,128)(2,1)S(1)}, bf16[2,512,1,128]{3,1,2,0:T(8,128)(2,1)S(1)}, u32[]{:S(2)}, u32[]{:S(2)}) collective-permute-start(bf16[2,512,1,128]{3,1,2,0:T(8,128)(2,1)S(1)} %copy.49), channel_id=1, source_target_pairs={{0,8},{8,16},{16,24},{24,32},{32,40},{40,48},{48,56},{56,64},{64,7... | collective-permute-start | bytes 786440 | tf_op jit(solution)/shard_map/while/body/eval_jaxpr/ppermute | solution.py:13
  393.0 15.4 %collective-permute-start.1 = (f32[2,512,1,128]{3,1,2,0:T(8,128)S(1)}, f32[2,512,1,128]{3,1,2,0:T(8,128)S(1)}, u32[]{:S(2)}, u32[]{:S(2)}) collective-permute-start(f32[2,512,1,128]{3,1,2,0:T(8,128)S(1)} %convert_add_fusion.3), channel_id=1, source_target_pairs={{0,8},{8,16},{16,24},{24,32},{32,40},{40,48},{48,56},{56,64},{64,7... | collective-permute-start | bytes 1572872 | tf_op jit(solution)/shard_map/while/body/eval_jaxpr/ppermute | solution.py:13
  393.0 15.3 %collective-permute-start = (bf16[2,512,1,128]{3,1,2,0:T(8,128)(2,1)S(1)}, bf16[2,512,1,128]{3,1,2,0:T(8,128)(2,1)S(1)}, u32[]{:S(2)}, u32[]{:S(2)}) collective-permute-start(bf16[2,512,1,128]{3,1,2,0:T(8,128)(2,1)S(1)} %copy.49), channel_id=1, source_target_pairs={{0,8},{8,16},{16,24},{24,32},{32,40},{40,48},{48,56},{56,64},{64,7... | collective-permute-start | bytes 786440 | tf_op jit(solution)/shard_map/while/body/eval_jaxpr/ppermute | solution.py:13
  412.4 15.4 %collective-permute-start.1 = (f32[2,512,1,128]{3,1,2,0:T(8,128)S(1)}, f32[2,512,1,128]{3,1,2,0:T(8,128)S(1)}, u32[]{:S(2)}, u32[]{:S(2)}) collective-permute-start(f32[2,512,1,128]{3,1,2,0:T(8,128)S(1)} %convert_add_fusion.3), channel_id=1, source_target_pairs={{0,8},{8,16},{16,24},{24,32},{32,40},{40,48},{48,56},{56,64},{64,7... | collective-permute-start | bytes 1572872 | tf_op jit(solution)/shard_map/while/body/eval_jaxpr/ppermute | solution.py:13
  412.5 15.3 %collective-permute-start = (bf16[2,512,1,128]{3,1,2,0:T(8,128)(2,1)S(1)}, bf16[2,512,1,128]{3,1,2,0:T(8,128)(2,1)S(1)}, u32[]{:S(2)}, u32[]{:S(2)}) collective-permute-start(bf16[2,512,1,128]{3,1,2,0:T(8,128)(2,1)S(1)} %copy.49), channel_id=1, source_target_pairs={{0,8},{8,16},{16,24},{24,32},{32,40},{40,48},{48,56},{56,64},{64,7... | collective-permute-start | bytes 786440 | tf_op jit(solution)/shard_map/while/body/eval_jaxpr/ppermute | solution.py:13
  431.9 15.4 %collective-permute-start.1 = (f32[2,512,1,128]{3,1,2,0:T(8,128)S(1)}, f32[2,512,1,128]{3,1,2,0:T(8,128)S(1)}, u32[]{:S(2)}, u32[]{:S(2)}) collective-permute-start(f32[2,512,1,128]{3,1,2,0:T(8,128)S(1)} %convert_add_fusion.3), channel_id=1, source_target_pairs={{0,8},{8,16},{16,24},{24,32},{32,40},{40,48},{48,56},{56,64},{64,7... | collective-permute-start | bytes 1572872 | tf_op jit(solution)/shard_map/while/body/eval_jaxpr/ppermute | solution.py:13
  432.0 15.3 %collective-permute-start = (bf16[2,512,1,128]{3,1,2,0:T(8,128)(2,1)S(1)}, bf16[2,512,1,128]{3,1,2,0:T(8,128)(2,1)S(1)}, u32[]{:S(2)}, u32[]{:S(2)}) collective-permute-start(bf16[2,512,1,128]{3,1,2,0:T(8,128)(2,1)S(1)} %copy.49), channel_id=1, source_target_pairs={{0,8},{8,16},{16,24},{24,32},{32,40},{40,48},{48,56},{56,64},{64,7... | collective-permute-start | bytes 786440 | tf_op jit(solution)/shard_map/while/body/eval_jaxpr/ppermute | solution.py:13
  451.4 15.4 %collective-permute-start.1 = (f32[2,512,1,128]{3,1,2,0:T(8,128)S(1)}, f32[2,512,1,128]{3,1,2,0:T(8,128)S(1)}, u32[]{:S(2)}, u32[]{:S(2)}) collective-permute-start(f32[2,512,1,128]{3,1,2,0:T(8,128)S(1)} %convert_add_fusion.3), channel_id=1, source_target_pairs={{0,8},{8,16},{16,24},{24,32},{32,40},{40,48},{48,56},{56,64},{64,7... | collective-permute-start | bytes 1572872 | tf_op jit(solution)/shard_map/while/body/eval_jaxpr/ppermute | solution.py:13
  470.9 15.4 %collective-permute-start.1 = (f32[2,512,1,128]{3,1,2,0:T(8,128)S(1)}, f32[2,512,1,128]{3,1,2,0:T(8,128)S(1)}, u32[]{:S(2)}, u32[]{:S(2)}) collective-permute-start(f32[2,512,1,128]{3,1,2,0:T(8,128)S(1)} %convert_add_fusion.3), channel_id=1, source_target_pairs={{0,8},{8,16},{16,24},{24,32},{32,40},{40,48},{48,56},{56,64},{64,7... | collective-permute-start | bytes 1572872 | tf_op jit(solution)/shard_map/while/body/eval_jaxpr/ppermute | solution.py:13
  471.0 15.3 %collective-permute-start = (bf16[2,512,1,128]{3,1,2,0:T(8,128)(2,1)S(1)}, bf16[2,512,1,128]{3,1,2,0:T(8,128)(2,1)S(1)}, u32[]{:S(2)}, u32[]{:S(2)}) collective-permute-start(bf16[2,512,1,128]{3,1,2,0:T(8,128)(2,1)S(1)} %copy.49), channel_id=1, source_target_pairs={{0,8},{8,16},{16,24},{24,32},{32,40},{40,48},{48,56},{56,64},{64,7... | collective-permute-start | bytes 786440 | tf_op jit(solution)/shard_map/while/body/eval_jaxpr/ppermute | solution.py:13
  490.4 15.4 %collective-permute-start.1 = (f32[2,512,1,128]{3,1,2,0:T(8,128)S(1)}, f32[2,512,1,128]{3,1,2,0:T(8,128)S(1)}, u32[]{:S(2)}, u32[]{:S(2)}) collective-permute-start(f32[2,512,1,128]{3,1,2,0:T(8,128)S(1)} %convert_add_fusion.3), channel_id=1, source_target_pairs={{0,8},{8,16},{16,24},{24,32},{32,40},{40,48},{48,56},{56,64},{64,7... | collective-permute-start | bytes 1572872 | tf_op jit(solution)/shard_map/while/body/eval_jaxpr/ppermute | solution.py:13
  509.8 15.4 %collective-permute-start.1 = (f32[2,512,1,128]{3,1,2,0:T(8,128)S(1)}, f32[2,512,1,128]{3,1,2,0:T(8,128)S(1)}, u32[]{:S(2)}, u32[]{:S(2)}) collective-permute-start(f32[2,512,1,128]{3,1,2,0:T(8,128)S(1)} %convert_add_fusion.3), channel_id=1, source_target_pairs={{0,8},{8,16},{16,24},{24,32},{32,40},{40,48},{48,56},{56,64},{64,7... | collective-permute-start | bytes 1572872 | tf_op jit(solution)/shard_map/while/body/eval_jaxpr/ppermute | solution.py:13
  509.9 15.3 %collective-permute-start = (bf16[2,512,1,128]{3,1,2,0:T(8,128)(2,1)S(1)}, bf16[2,512,1,128]{3,1,2,0:T(8,128)(2,1)S(1)}, u32[]{:S(2)}, u32[]{:S(2)}) collective-permute-start(bf16[2,512,1,128]{3,1,2,0:T(8,128)(2,1)S(1)} %copy.49), channel_id=1, source_target_pairs={{0,8},{8,16},{16,24},{24,32},{32,40},{40,48},{48,56},{56,64},{64,7... | collective-permute-start | bytes 786440 | tf_op jit(solution)/shard_map/while/body/eval_jaxpr/ppermute | solution.py:13
  529.3 15.4 %collective-permute-start.1 = (f32[2,512,1,128]{3,1,2,0:T(8,128)S(1)}, f32[2,512,1,128]{3,1,2,0:T(8,128)S(1)}, u32[]{:S(2)}, u32[]{:S(2)}) collective-permute-start(f32[2,512,1,128]{3,1,2,0:T(8,128)S(1)} %convert_add_fusion.3), channel_id=1, source_target_pairs={{0,8},{8,16},{16,24},{24,32},{32,40},{40,48},{48,56},{56,64},{64,7... | collective-permute-start | bytes 1572872 | tf_op jit(solution)/shard_map/while/body/eval_jaxpr/ppermute | solution.py:13
  548.8 15.4 %collective-permute-start.1 = (f32[2,512,1,128]{3,1,2,0:T(8,128)S(1)}, f32[2,512,1,128]{3,1,2,0:T(8,128)S(1)}, u32[]{:S(2)}, u32[]{:S(2)}) collective-permute-start(f32[2,512,1,128]{3,1,2,0:T(8,128)S(1)} %convert_add_fusion.3), channel_id=1, source_target_pairs={{0,8},{8,16},{16,24},{24,32},{32,40},{40,48},{48,56},{56,64},{64,7... | collective-permute-start | bytes 1572872 | tf_op jit(solution)/shard_map/while/body/eval_jaxpr/ppermute | solution.py:13
  548.9 15.3 %collective-permute-start = (bf16[2,512,1,128]{3,1,2,0:T(8,128)(2,1)S(1)}, bf16[2,512,1,128]{3,1,2,0:T(8,128)(2,1)S(1)}, u32[]{:S(2)}, u32[]{:S(2)}) collective-permute-start(bf16[2,512,1,128]{3,1,2,0:T(8,128)(2,1)S(1)} %copy.49), channel_id=1, source_target_pairs={{0,8},{8,16},{16,24},{24,32},{32,40},{40,48},{48,56},{56,64},{64,7... | collective-permute-start | bytes 786440 | tf_op jit(solution)/shard_map/while/body/eval_jaxpr/ppermute | solution.py:13
  568.3 15.4 %collective-permute-start.1 = (f32[2,512,1,128]{3,1,2,0:T(8,128)S(1)}, f32[2,512,1,128]{3,1,2,0:T(8,128)S(1)}, u32[]{:S(2)}, u32[]{:S(2)}) collective-permute-start(f32[2,512,1,128]{3,1,2,0:T(8,128)S(1)} %convert_add_fusion.3), channel_id=1, source_target_pairs={{0,8},{8,16},{16,24},{24,32},{32,40},{40,48},{48,56},{56,64},{64,7... | collective-permute-start | bytes 1572872 | tf_op jit(solution)/shard_map/while/body/eval_jaxpr/ppermute | solution.py:13
  587.8 15.4 %collective-permute-start.1 = (f32[2,512,1,128]{3,1,2,0:T(8,128)S(1)}, f32[2,512,1,128]{3,1,2,0:T(8,128)S(1)}, u32[]{:S(2)}, u32[]{:S(2)}) collective-permute-start(f32[2,512,1,128]{3,1,2,0:T(8,128)S(1)} %convert_add_fusion.3), channel_id=1, source_target_pairs={{0,8},{8,16},{16,24},{24,32},{32,40},{40,48},{48,56},{56,64},{64,7... | collective-permute-start | bytes 1572872 | tf_op jit(solution)/shard_map/while/body/eval_jaxpr/ppermute | solution.py:13
  587.9 15.3 %collective-permute-start = (bf16[2,512,1,128]{3,1,2,0:T(8,128)(2,1)S(1)}, bf16[2,512,1,128]{3,1,2,0:T(8,128)(2,1)S(1)}, u32[]{:S(2)}, u32[]{:S(2)}) collective-permute-start(bf16[2,512,1,128]{3,1,2,0:T(8,128)(2,1)S(1)} %copy.49), channel_id=1, source_target_pairs={{0,8},{8,16},{16,24},{24,32},{32,40},{40,48},{48,56},{56,64},{64,7... | collective-permute-start | bytes 786440 | tf_op jit(solution)/shard_map/while/body/eval_jaxpr/ppermute | solution.py:13
  607.3 15.4 %collective-permute-start.1 = (f32[2,512,1,128]{3,1,2,0:T(8,128)S(1)}, f32[2,512,1,128]{3,1,2,0:T(8,128)S(1)}, u32[]{:S(2)}, u32[]{:S(2)}) collective-permute-start(f32[2,512,1,128]{3,1,2,0:T(8,128)S(1)} %convert_add_fusion.3), channel_id=1, source_target_pairs={{0,8},{8,16},{16,24},{24,32},{32,40},{40,48},{48,56},{56,64},{64,7... | collective-permute-start | bytes 1572872 | tf_op jit(solution)/shard_map/while/body/eval_jaxpr/ppermute | solution.py:13
  626.7 15.4 %collective-permute-start.1 = (f32[2,512,1,128]{3,1,2,0:T(8,128)S(1)}, f32[2,512,1,128]{3,1,2,0:T(8,128)S(1)}, u32[]{:S(2)}, u32[]{:S(2)}) collective-permute-start(f32[2,512,1,128]{3,1,2,0:T(8,128)S(1)} %convert_add_fusion.3), channel_id=1, source_target_pairs={{0,8},{8,16},{16,24},{24,32},{32,40},{40,48},{48,56},{56,64},{64,7... | collective-permute-start | bytes 1572872 | tf_op jit(solution)/shard_map/while/body/eval_jaxpr/ppermute | solution.py:13
  626.8 15.3 %collective-permute-start = (bf16[2,512,1,128]{3,1,2,0:T(8,128)(2,1)S(1)}, bf16[2,512,1,128]{3,1,2,0:T(8,128)(2,1)S(1)}, u32[]{:S(2)}, u32[]{:S(2)}) collective-permute-start(bf16[2,512,1,128]{3,1,2,0:T(8,128)(2,1)S(1)} %copy.49), channel_id=1, source_target_pairs={{0,8},{8,16},{16,24},{24,32},{32,40},{40,48},{48,56},{56,64},{64,7... | collective-permute-start | bytes 786440 | tf_op jit(solution)/shard_map/while/body/eval_jaxpr/ppermute | solution.py:13
  646.2 15.4 %collective-permute-start.1 = (f32[2,512,1,128]{3,1,2,0:T(8,128)S(1)}, f32[2,512,1,128]{3,1,2,0:T(8,128)S(1)}, u32[]{:S(2)}, u32[]{:S(2)}) collective-permute-start(f32[2,512,1,128]{3,1,2,0:T(8,128)S(1)} %convert_add_fusion.3), channel_id=1, source_target_pairs={{0,8},{8,16},{16,24},{24,32},{32,40},{40,48},{48,56},{56,64},{64,7... | collective-permute-start | bytes 1572872 | tf_op jit(solution)/shard_map/while/body/eval_jaxpr/ppermute | solution.py:13
  (23 other events, 1042.2 us)
Sparse Core Ops, SparseCore 0:
  9.8 64.3 all-gather.1
  675.3 106.6 reduce-scatter.1
where the time goes:
time: 792 us; the launch traced here: 790 us
  waiting for transfers between devices  612 us (77%)
  local copies, waits for them, and re-layouts  79.1 us (10%)
  matrix products  63.9 us (8%)
  between operations  13.6 us (2%)
  starting transfers between devices  13.3 us (2%)
    ppermute x63, waiting for transfers between devices, from_behind(): lax.ppermute(value, axis, [(i, (i + by) % count) for i in range(count)])  442 us
    reduce_scatter x1, waiting for transfers between devices, per_device(): lax.psum_scatter(total + lax.dot_general(w_value, d_value, contract, pref...  107 us
    all_gather x1, waiting for transfers between devices, per_device(): lax.all_gather(out_grad, 'head', axis=1, tiled=True)  61.9 us
    broadcast_in_dim x31, local copies, waits for them, and re-layouts, visit(): jnp.repeat(jnp.repeat(listed, TILE, axis=0), TILE, axis=1)  49.5 us
    dynamic_slice x32, local copies, waits for them, and re-layouts, visit(): lax.dynamic_slice_in_dim(trace_id, first_tile * TILE, key_block.shape[0], 0)  24.4 us
  transfers between devices with their start and end apart: 65, of which 34 were waited for; matrix products, arithmetic and copies ran while one was open for 2% of the time, Pallas kernels for 0%

commit v1 on v0

--- a/solution.py
+++ b/solution.py
@@ -6,6 +6,11 @@
 HD = 128
 TILE = 128
 SEL = 48
+
+
+def all_by_exchange(x, name, d):
+    sent = jnp.stack([x] * lax.axis_size(name))
+    return jnp.concatenate(lax.all_to_all(sent, name, 0, 0), axis=d)
 
 
 def from_behind(value, axis, by):
@@ -62,7 +67,7 @@
     seq_index = lax.axis_index("seq")
     tiles_here = tokens_here // TILE
     d_attn = lax.dot_general(
-        lax.all_gather(out_grad, "head", axis=1, tiled=True),
+        all_by_exchange(out_grad, "head", 1),
         w_out,
         (((1,), (1,)), ((), ())),
         preferred_element_type=jnp.float32,

time: 792 us -> 763 us (0.963)
  waiting for transfers between devices: 612 us -> 574 us
  starting transfers between devices: 13.3 us -> 24.8 us
    all_gather x1 -> x0, waiting for transfers between devices: 61.9 us -> none  [per_device(): lax.all_gather(out_grad, 'head', axis=1, tiled=True)]
    all_to_all x0 -> x1, waiting for transfers between devices: none -> 20.1 us  [all_by_exchange(): return jnp.concatenate(lax.all_to_all(sent, name, 0, 0), axis=d)]
    all_to_all x0 -> x1, starting transfers between devices: none -> 10.9 us  [all_by_exchange(): return jnp.concatenate(lax.all_to_all(sent, name, 0, 0), axis=d)]
where the time goes in v1:
time: 763 us; the launch traced here: 761 us
  waiting for transfers between devices  574 us (75%)
  local copies, waits for them, and re-layouts  80.4 us (11%)
  matrix products  62.5 us (8%)
  starting transfers between devices  24.8 us (3%)
  between operations  13.7 us (2%)
    ppermute x63, waiting for transfers between devices, from_behind(): lax.ppermute(value, axis, [(i, (i + by) % count) for i in range(count)])  442 us
    reduce_scatter x1, waiting for transfers between devices, per_device(): lax.psum_scatter(total + lax.dot_general(w_value, d_value, contract, pref...  112 us
    broadcast_in_dim x31, local copies, waits for them, and re-layouts, visit(): jnp.repeat(jnp.repeat(listed, TILE, axis=0), TILE, axis=1)  49.5 us
    dynamic_slice x32, local copies, waits for them, and re-layouts, visit(): lax.dynamic_slice_in_dim(trace_id, first_tile * TILE, key_block.shape[0], 0)  24.4 us
    all_to_all x1, waiting for transfers between devices, all_by_exchange(): return jnp.concatenate(lax.all_to_all(sent, name, 0, 0), axis=d)  20.1 us
    dot_general x32, matrix products, pair_grads(): jnp.einsum('rhd,chd->hrc', query_heads, key_heads, preferred_element_type...  15.7 us
  transfers between devices with their start and end apart: 65, of which 34 were waited for; matrix products, arithmetic and copies ran while one was open for 2% of the time, Pallas kernels for 0%

profile of v1, /device:TPU:8, one launch (start us, length us, event | category | flops | bytes accessed | tf_op | source)
XLA Modules:
  0.0 761.5 jit_solution(18106558988705984346)
XLA Ops:
  8.7 10.9 %all-to-all-start = ((bf16[8,512,128]{1,2,0:T(8,128)(2,1)}), bf16[8,512,128]{1,2,0:T(8,128)(2,1)S(1)}, u32[]{:S(2)}, u32[]{:S(2)}) async-start(bf16[8,512,128]{1,2,0:T(8,128)(2,1)} %stack.68), calls=%async_computation | async-start | bytes 2097152 | tf_op jit(solution)/shard_map/all_to_all | solution.py:13
  21.5 20.1 %all-to-all-done = bf16[8,512,128]{1,2,0:T(8,128)(2,1)S(1)} async-done(((bf16[8,512,128]{1,2,0:T(8,128)(2,1)}), bf16[8,512,128]{1,2,0:T(8,128)(2,1)S(1)}, u32[]{:S(2)}, u32[]{:S(2)}) %all-to-all-start) | async-done | bytes 1048608 | tf_op jit(solution)/shard_map/all_to_all | solution.py:13
  42.1 585.4 %while.20 = (s32[]{:T(128)}, bf16[2,512,1,128]{3,1,2,0:T(8,128)(2,1)S(1)}, f32[2,512,1,128]{3,1,2,0:T(8,128)S(1)}, f32[512,1,128]{2,0,1:T(8,128)S(1)}, s32[]{:T(...) while((s32[]{:T(128)}, ...), condition=%wide.region_3.4_spmd.clone, body=%wide.region_2.3_spmd.clone.sunk | while | flops 338821152 | bytes 11944476 | solution.py:118
  46.3 1.7 collective-permute-start
  48.3 9.4 %collective-permute-done = bf16[2,512,1,128]{3,1,2,0:T(8,128)(2,1)S(1)} collective-permute-done((bf16[2,512,1,128]{3,1,2,0:T(8,128)(2,1)S(1)}, bf16[2,512,1,128]{3,1,2,0:T(8,128)(2,1)S(1)}, u32[]{:S(2)}, u32[]{:S(2)}) %collective-permute-start) | collective-permute-done | bytes 262176 | tf_op jit(solution)/shard_map/while/body/eval_jaxpr/ppermute | solution.py:18
  58.6 1.6 broadcast_in_dim.75
  61.9 1.7 collective-permute-start
  63.9 9.4 %collective-permute-done = bf16[2,512,1,128]{3,1,2,0:T(8,128)(2,1)S(1)} collective-permute-done((bf16[2,512,1,128]{3,1,2,0:T(8,128)(2,1)S(1)}, bf16[2,512,1,128]{3,1,2,0:T(8,128)(2,1)S(1)}, u32[]{:S(2)}, u32[]{:S(2)}) %collective-permute-start) | collective-permute-done | bytes 262176 | tf_op jit(solution)/shard_map/while/body/eval_jaxpr/ppermute | solution.py:18
  74.2 1.6 broadcast_in_dim.75
  77.5 1.7 collective-permute-start
  79.5 9.4 %collective-permute-done = bf16[2,512,1,128]{3,1,2,0:T(8,128)(2,1)S(1)} collective-permute-done((bf16[2,512,1,128]{3,1,2,0:T(8,128)(2,1)S(1)}, bf16[2,512,1,128]{3,1,2,0:T(8,128)(2,1)S(1)}, u32[]{:S(2)}, u32[]{:S(2)}) %collective-permute-start) | collective-permute-done | bytes 262176 | tf_op jit(solution)/shard_map/while/body/eval_jaxpr/ppermute | solution.py:18
  89.8 1.6 broadcast_in_dim.75
  93.1 1.7 collective-permute-start
  95.1 9.4 %collective-permute-done = bf16[2,512,1,128]{3,1,2,0:T(8,128)(2,1)S(1)} collective-permute-done((bf16[2,512,1,128]{3,1,2,0:T(8,128)(2,1)S(1)}, bf16[2,512,1,128]{3,1,2,0:T(8,128)(2,1)S(1)}, u32[]{:S(2)}, u32[]{:S(2)}) %collective-permute-start) | collective-permute-done | bytes 262176 | tf_op jit(solution)/shard_map/while/body/eval_jaxpr/ppermute | solution.py:18
  105.4 1.6 broadcast_in_dim.75
  108.6 1.7 collective-permute-start
  110.6 10.3 %collective-permute-done = bf16[2,512,1,128]{3,1,2,0:T(8,128)(2,1)S(1)} collective-permute-done((bf16[2,512,1,128]{3,1,2,0:T(8,128)(2,1)S(1)}, bf16[2,512,1,128]{3,1,2,0:T(8,128)(2,1)S(1)}, u32[]{:S(2)}, u32[]{:S(2)}) %collective-permute-start) | collective-permute-done | bytes 262176 | tf_op jit(solution)/shard_map/while/body/eval_jaxpr/ppermute | solution.py:18
  126.2 14.2 %collective-permute-done = bf16[2,512,1,128]{3,1,2,0:T(8,128)(2,1)S(1)} collective-permute-done((bf16[2,512,1,128]{3,1,2,0:T(8,128)(2,1)S(1)}, bf16[2,512,1,128]{3,1,2,0:T(8,128)(2,1)S(1)}, u32[]{:S(2)}, u32[]{:S(2)}) %collective-permute-start) | collective-permute-done | bytes 262176 | tf_op jit(solution)/shard_map/while/body/eval_jaxpr/ppermute | solution.py:18
  145.0 14.9 %collective-permute-done = bf16[2,512,1,128]{3,1,2,0:T(8,128)(2,1)S(1)} collective-permute-done((bf16[2,512,1,128]{3,1,2,0:T(8,128)(2,1)S(1)}, bf16[2,512,1,128]{3,1,2,0:T(8,128)(2,1)S(1)}, u32[]{:S(2)}, u32[]{:S(2)}) %collective-permute-start) | collective-permute-done | bytes 262176 | tf_op jit(solution)/shard_map/while/body/eval_jaxpr/ppermute | solution.py:18
  164.5 14.9 %collective-permute-done = bf16[2,512,1,128]{3,1,2,0:T(8,128)(2,1)S(1)} collective-permute-done((bf16[2,512,1,128]{3,1,2,0:T(8,128)(2,1)S(1)}, bf16[2,512,1,128]{3,1,2,0:T(8,128)(2,1)S(1)}, u32[]{:S(2)}, u32[]{:S(2)}) %collective-permute-start) | collective-permute-done | bytes 262176 | tf_op jit(solution)/shard_map/while/body/eval_jaxpr/ppermute | solution.py:18
  184.0 14.9 %collective-permute-done = bf16[2,512,1,128]{3,1,2,0:T(8,128)(2,1)S(1)} collective-permute-done((bf16[2,512,1,128]{3,1,2,0:T(8,128)(2,1)S(1)}, bf16[2,512,1,128]{3,1,2,0:T(8,128)(2,1)S(1)}, u32[]{:S(2)}, u32[]{:S(2)}) %collective-permute-start) | collective-permute-done | bytes 262176 | tf_op jit(solution)/shard_map/while/body/eval_jaxpr/ppermute | solution.py:18
  203.5 14.9 %collective-permute-done = bf16[2,512,1,128]{3,1,2,0:T(8,128)(2,1)S(1)} collective-permute-done((bf16[2,512,1,128]{3,1,2,0:T(8,128)(2,1)S(1)}, bf16[2,512,1,128]{3,1,2,0:T(8,128)(2,1)S(1)}, u32[]{:S(2)}, u32[]{:S(2)}) %collective-permute-start) | collective-permute-done | bytes 262176 | tf_op jit(solution)/shard_map/while/body/eval_jaxpr/ppermute | solution.py:18
  223.0 14.9 %collective-permute-done = bf16[2,512,1,128]{3,1,2,0:T(8,128)(2,1)S(1)} collective-permute-done((bf16[2,512,1,128]{3,1,2,0:T(8,128)(2,1)S(1)}, bf16[2,512,1,128]{3,1,2,0:T(8,128)(2,1)S(1)}, u32[]{:S(2)}, u32[]{:S(2)}) %collective-permute-start) | collective-permute-done | bytes 262176 | tf_op jit(solution)/shard_map/while/body/eval_jaxpr/ppermute | solution.py:18
  242.4 14.9 %collective-permute-done = bf16[2,512,1,128]{3,1,2,0:T(8,128)(2,1)S(1)} collective-permute-done((bf16[2,512,1,128]{3,1,2,0:T(8,128)(2,1)S(1)}, bf16[2,512,1,128]{3,1,2,0:T(8,128)(2,1)S(1)}, u32[]{:S(2)}, u32[]{:S(2)}) %collective-permute-start) | collective-permute-done | bytes 262176 | tf_op jit(solution)/shard_map/while/body/eval_jaxpr/ppermute | solution.py:18
  261.9 14.9 %collective-permute-done = bf16[2,512,1,128]{3,1,2,0:T(8,128)(2,1)S(1)} collective-permute-done((bf16[2,512,1,128]{3,1,2,0:T(8,128)(2,1)S(1)}, bf16[2,512,1,128]{3,1,2,0:T(8,128)(2,1)S(1)}, u32[]{:S(2)}, u32[]{:S(2)}) %collective-permute-start) | collective-permute-done | bytes 262176 | tf_op jit(solution)/shard_map/while/body/eval_jaxpr/ppermute | solution.py:18
  281.4 14.9 %collective-permute-done = bf16[2,512,1,128]{3,1,2,0:T(8,128)(2,1)S(1)} collective-permute-done((bf16[2,512,1,128]{3,1,2,0:T(8,128)(2,1)S(1)}, bf16[2,512,1,128]{3,1,2,0:T(8,128)(2,1)S(1)}, u32[]{:S(2)}, u32[]{:S(2)}) %collective-permute-start) | collective-permute-done | bytes 262176 | tf_op jit(solution)/shard_map/while/body/eval_jaxpr/ppermute | solution.py:18
  300.9 14.9 %collective-permute-done = bf16[2,512,1,128]{3,1,2,0:T(8,128)(2,1)S(1)} collective-permute-done((bf16[2,512,1,128]{3,1,2,0:T(8,128)(2,1)S(1)}, bf16[2,512,1,128]{3,1,2,0:T(8,128)(2,1)S(1)}, u32[]{:S(2)}, u32[]{:S(2)}) %collective-permute-start) | collective-permute-done | bytes 262176 | tf_op jit(solution)/shard_map/while/body/eval_jaxpr/ppermute | solution.py:18
  320.4 14.9 %collective-permute-done = bf16[2,512,1,128]{3,1,2,0:T(8,128)(2,1)S(1)} collective-permute-done((bf16[2,512,1,128]{3,1,2,0:T(8,128)(2,1)S(1)}, bf16[2,512,1,128]{3,1,2,0:T(8,128)(2,1)S(1)}, u32[]{:S(2)}, u32[]{:S(2)}) %collective-permute-start) | collective-permute-done | bytes 262176 | tf_op jit(solution)/shard_map/while/body/eval_jaxpr/ppermute | solution.py:18
  339.9 14.9 %collective-permute-done = bf16[2,512,1,128]{3,1,2,0:T(8,128)(2,1)S(1)} collective-permute-done((bf16[2,512,1,128]{3,1,2,0:T(8,128)(2,1)S(1)}, bf16[2,512,1,128]{3,1,2,0:T(8,128)(2,1)S(1)}, u32[]{:S(2)}, u32[]{:S(2)}) %collective-permute-start) | collective-permute-done | bytes 262176 | tf_op jit(solution)/shard_map/while/body/eval_jaxpr/ppermute | solution.py:18
  359.3 14.9 %collective-permute-done = bf16[2,512,1,128]{3,1,2,0:T(8,128)(2,1)S(1)} collective-permute-done((bf16[2,512,1,128]{3,1,2,0:T(8,128)(2,1)S(1)}, bf16[2,512,1,128]{3,1,2,0:T(8,128)(2,1)S(1)}, u32[]{:S(2)}, u32[]{:S(2)}) %collective-permute-start) | collective-permute-done | bytes 262176 | tf_op jit(solution)/shard_map/while/body/eval_jaxpr/ppermute | solution.py:18
  378.8 14.9 %collective-permute-done = bf16[2,512,1,128]{3,1,2,0:T(8,128)(2,1)S(1)} collective-permute-done((bf16[2,512,1,128]{3,1,2,0:T(8,128)(2,1)S(1)}, bf16[2,512,1,128]{3,1,2,0:T(8,128)(2,1)S(1)}, u32[]{:S(2)}, u32[]{:S(2)}) %collective-permute-start) | collective-permute-done | bytes 262176 | tf_op jit(solution)/shard_map/while/body/eval_jaxpr/ppermute | solution.py:18
  398.3 14.9 %collective-permute-done = bf16[2,512,1,128]{3,1,2,0:T(8,128)(2,1)S(1)} collective-permute-done((bf16[2,512,1,128]{3,1,2,0:T(8,128)(2,1)S(1)}, bf16[2,512,1,128]{3,1,2,0:T(8,128)(2,1)S(1)}, u32[]{:S(2)}, u32[]{:S(2)}) %collective-permute-start) | collective-permute-done | bytes 262176 | tf_op jit(solution)/shard_map/while/body/eval_jaxpr/ppermute | solution.py:18
  417.8 14.9 %collective-permute-done = bf16[2,512,1,128]{3,1,2,0:T(8,128)(2,1)S(1)} collective-permute-done((bf16[2,512,1,128]{3,1,2,0:T(8,128)(2,1)S(1)}, bf16[2,512,1,128]{3,1,2,0:T(8,128)(2,1)S(1)}, u32[]{:S(2)}, u32[]{:S(2)}) %collective-permute-start) | collective-permute-done | bytes 262176 | tf_op jit(solution)/shard_map/while/body/eval_jaxpr/ppermute | solution.py:18
  437.3 14.9 %collective-permute-done = bf16[2,512,1,128]{3,1,2,0:T(8,128)(2,1)S(1)} collective-permute-done((bf16[2,512,1,128]{3,1,2,0:T(8,128)(2,1)S(1)}, bf16[2,512,1,128]{3,1,2,0:T(8,128)(2,1)S(1)}, u32[]{:S(2)}, u32[]{:S(2)}) %collective-permute-start) | collective-permute-done | bytes 262176 | tf_op jit(solution)/shard_map/while/body/eval_jaxpr/ppermute | solution.py:18
  456.8 14.9 %collective-permute-done = bf16[2,512,1,128]{3,1,2,0:T(8,128)(2,1)S(1)} collective-permute-done((bf16[2,512,1,128]{3,1,2,0:T(8,128)(2,1)S(1)}, bf16[2,512,1,128]{3,1,2,0:T(8,128)(2,1)S(1)}, u32[]{:S(2)}, u32[]{:S(2)}) %collective-permute-start) | collective-permute-done | bytes 262176 | tf_op jit(solution)/shard_map/while/body/eval_jaxpr/ppermute | solution.py:18
  476.2 14.9 %collective-permute-done = bf16[2,512,1,128]{3,1,2,0:T(8,128)(2,1)S(1)} collective-permute-done((bf16[2,512,1,128]{3,1,2,0:T(8,128)(2,1)S(1)}, bf16[2,512,1,128]{3,1,2,0:T(8,128)(2,1)S(1)}, u32[]{:S(2)}, u32[]{:S(2)}) %collective-permute-start) | collective-permute-done | bytes 262176 | tf_op jit(solution)/shard_map/while/body/eval_jaxpr/ppermute | solution.py:18
  495.7 14.9 %collective-permute-done = bf16[2,512,1,128]{3,1,2,0:T(8,128)(2,1)S(1)} collective-permute-done((bf16[2,512,1,128]{3,1,2,0:T(8,128)(2,1)S(1)}, bf16[2,512,1,128]{3,1,2,0:T(8,128)(2,1)S(1)}, u32[]{:S(2)}, u32[]{:S(2)}) %collective-permute-start) | collective-permute-done | bytes 262176 | tf_op jit(solution)/shard_map/while/body/eval_jaxpr/ppermute | solution.py:18
  515.2 14.9 %collective-permute-done = bf16[2,512,1,128]{3,1,2,0:T(8,128)(2,1)S(1)} collective-permute-done((bf16[2,512,1,128]{3,1,2,0:T(8,128)(2,1)S(1)}, bf16[2,512,1,128]{3,1,2,0:T(8,128)(2,1)S(1)}, u32[]{:S(2)}, u32[]{:S(2)}) %collective-permute-start) | collective-permute-done | bytes 262176 | tf_op jit(solution)/shard_map/while/body/eval_jaxpr/ppermute | solution.py:18
  534.7 14.9 %collective-permute-done = bf16[2,512,1,128]{3,1,2,0:T(8,128)(2,1)S(1)} collective-permute-done((bf16[2,512,1,128]{3,1,2,0:T(8,128)(2,1)S(1)}, bf16[2,512,1,128]{3,1,2,0:T(8,128)(2,1)S(1)}, u32[]{:S(2)}, u32[]{:S(2)}) %collective-permute-start) | collective-permute-done | bytes 262176 | tf_op jit(solution)/shard_map/while/body/eval_jaxpr/ppermute | solution.py:18
  554.2 14.9 %collective-permute-done = bf16[2,512,1,128]{3,1,2,0:T(8,128)(2,1)S(1)} collective-permute-done((bf16[2,512,1,128]{3,1,2,0:T(8,128)(2,1)S(1)}, bf16[2,512,1,128]{3,1,2,0:T(8,128)(2,1)S(1)}, u32[]{:S(2)}, u32[]{:S(2)}) %collective-permute-start) | collective-permute-done | bytes 262176 | tf_op jit(solution)/shard_map/while/body/eval_jaxpr/ppermute | solution.py:18
  573.6 14.9 %collective-permute-done = bf16[2,512,1,128]{3,1,2,0:T(8,128)(2,1)S(1)} collective-permute-done((bf16[2,512,1,128]{3,1,2,0:T(8,128)(2,1)S(1)}, bf16[2,512,1,128]{3,1,2,0:T(8,128)(2,1)S(1)}, u32[]{:S(2)}, u32[]{:S(2)}) %collective-permute-start) | collective-permute-done | bytes 262176 | tf_op jit(solution)/shard_map/while/body/eval_jaxpr/ppermute | solution.py:18
  593.1 14.9 %collective-permute-done = bf16[2,512,1,128]{3,1,2,0:T(8,128)(2,1)S(1)} collective-permute-done((bf16[2,512,1,128]{3,1,2,0:T(8,128)(2,1)S(1)}, bf16[2,512,1,128]{3,1,2,0:T(8,128)(2,1)S(1)}, u32[]{:S(2)}, u32[]{:S(2)}) %collective-permute-start) | collective-permute-done | bytes 262176 | tf_op jit(solution)/shard_map/while/body/eval_jaxpr/ppermute | solution.py:18
  612.6 14.9 %collective-permute-done = bf16[2,512,1,128]{3,1,2,0:T(8,128)(2,1)S(1)} collective-permute-done((bf16[2,512,1,128]{3,1,2,0:T(8,128)(2,1)S(1)}, bf16[2,512,1,128]{3,1,2,0:T(8,128)(2,1)S(1)}, u32[]{:S(2)}, u32[]{:S(2)}) %collective-permute-start) | collective-permute-done | bytes 262176 | tf_op jit(solution)/shard_map/while/body/eval_jaxpr/ppermute | solution.py:18
  629.1 2.0 fusion.32
  631.2 7.6 %collective-permute-done.2 = bf16[2,512,1,128]{3,1,2,0:T(8,128)(2,1)S(1)} collective-permute-done((bf16[2,512,1,128]{3,1,2,0:T(8,128)(2,1)S(1)}, bf16[2,512,1,128]{3,1,2,0:T(8,128)(2,1)S(1)}, u32[]{:S(2)}, u32[]{:S(2)}) %collective-permute-start.2) | collective-permute-done | bytes 262176 | tf_op jit(solution)/shard_map/ppermute | solution.py:18
  639.2 1.8 add_bitcast_fusion
  641.0 112.0 %reduce-scatter.2.cloned.1.call-done = f32[128,512]{0,1:T(8,128)} async-done(((f32[1024,512]{0,1:T(8,128)}), f32[128,512]{0,1:T(8,128)}) %reduce-scatter.2.cloned.1.call-update) | async-done | bytes 262160 | tf_op jit(solution)/shard_map/reduce_scatter | solution.py:128
  753.0 1.6 convert_bitcast_fusion
  (475 shorter events, 140.2 us)
Async XLA Ops:
  8.7 32.9 %all-to-all-start = ((bf16[8,512,128]{1,2,0:T(8,128)(2,1)}), bf16[8,512,128]{1,2,0:T(8,128)(2,1)S(1)}, u32[]{:S(2)}, u32[]{:S(2)}) async-start(bf16[8,512,128]{1,2,0:T(8,128)(2,1)} %stack.68), calls=%async_computation | async-start | bytes 2097152 | tf_op jit(solution)/shard_map/all_to_all | solution.py:13
  19.7 733.4 %reduce-scatter.2.cloned.1.call-start = ((), (), s32[]{:S(2)}) async-start(), calls=%async_computation.2 | async-start | bytes 2359296 | tf_op jit(solution)/shard_map/reduce_scatter | solution.py:128
  125.0 15.4 %collective-permute-start.1 = (f32[2,512,1,128]{3,1,2,0:T(8,128)S(1)}, f32[2,512,1,128]{3,1,2,0:T(8,128)S(1)}, u32[]{:S(2)}, u32[]{:S(2)}) collective-permute-start(f32[2,512,1,128]{3,1,2,0:T(8,128)S(1)} %convert_add_fusion.3), channel_id=1, source_target_pairs={{0,8},{8,16},{16,24},{24,32},{32,40},{40,48},{48,56},{56,64},{64,7... | collective-permute-start | bytes 1572872 | tf_op jit(solution)/shard_map/while/body/eval_jaxpr/ppermute | solution.py:18
  125.1 15.3 %collective-permute-start = (bf16[2,512,1,128]{3,1,2,0:T(8,128)(2,1)S(1)}, bf16[2,512,1,128]{3,1,2,0:T(8,128)(2,1)S(1)}, u32[]{:S(2)}, u32[]{:S(2)}) collective-permute-start(bf16[2,512,1,128]{3,1,2,0:T(8,128)(2,1)S(1)} %copy.51), channel_id=1, source_target_pairs={{0,8},{8,16},{16,24},{24,32},{32,40},{40,48},{48,56},{56,64},{64,7... | collective-permute-start | bytes 786440 | tf_op jit(solution)/shard_map/while/body/eval_jaxpr/ppermute | solution.py:18
  144.5 15.4 %collective-permute-start.1 = (f32[2,512,1,128]{3,1,2,0:T(8,128)S(1)}, f32[2,512,1,128]{3,1,2,0:T(8,128)S(1)}, u32[]{:S(2)}, u32[]{:S(2)}) collective-permute-start(f32[2,512,1,128]{3,1,2,0:T(8,128)S(1)} %convert_add_fusion.3), channel_id=1, source_target_pairs={{0,8},{8,16},{16,24},{24,32},{32,40},{40,48},{48,56},{56,64},{64,7... | collective-permute-start | bytes 1572872 | tf_op jit(solution)/shard_map/while/body/eval_jaxpr/ppermute | solution.py:18
  144.6 15.3 %collective-permute-start = (bf16[2,512,1,128]{3,1,2,0:T(8,128)(2,1)S(1)}, bf16[2,512,1,128]{3,1,2,0:T(8,128)(2,1)S(1)}, u32[]{:S(2)}, u32[]{:S(2)}) collective-permute-start(bf16[2,512,1,128]{3,1,2,0:T(8,128)(2,1)S(1)} %copy.51), channel_id=1, source_target_pairs={{0,8},{8,16},{16,24},{24,32},{32,40},{40,48},{48,56},{56,64},{64,7... | collective-permute-start | bytes 786440 | tf_op jit(solution)/shard_map/while/body/eval_jaxpr/ppermute | solution.py:18
  164.0 15.4 %collective-permute-start.1 = (f32[2,512,1,128]{3,1,2,0:T(8,128)S(1)}, f32[2,512,1,128]{3,1,2,0:T(8,128)S(1)}, u32[]{:S(2)}, u32[]{:S(2)}) collective-permute-start(f32[2,512,1,128]{3,1,2,0:T(8,128)S(1)} %convert_add_fusion.3), channel_id=1, source_target_pairs={{0,8},{8,16},{16,24},{24,32},{32,40},{40,48},{48,56},{56,64},{64,7... | collective-permute-start | bytes 1572872 | tf_op jit(solution)/shard_map/while/body/eval_jaxpr/ppermute | solution.py:18
  164.1 15.3 %collective-permute-start = (bf16[2,512,1,128]{3,1,2,0:T(8,128)(2,1)S(1)}, bf16[2,512,1,128]{3,1,2,0:T(8,128)(2,1)S(1)}, u32[]{:S(2)}, u32[]{:S(2)}) collective-permute-start(bf16[2,512,1,128]{3,1,2,0:T(8,128)(2,1)S(1)} %copy.51), channel_id=1, source_target_pairs={{0,8},{8,16},{16,24},{24,32},{32,40},{40,48},{48,56},{56,64},{64,7... | collective-permute-start | bytes 786440 | tf_op jit(solution)/shard_map/while/body/eval_jaxpr/ppermute | solution.py:18
  183.5 15.4 %collective-permute-start.1 = (f32[2,512,1,128]{3,1,2,0:T(8,128)S(1)}, f32[2,512,1,128]{3,1,2,0:T(8,128)S(1)}, u32[]{:S(2)}, u32[]{:S(2)}) collective-permute-start(f32[2,512,1,128]{3,1,2,0:T(8,128)S(1)} %convert_add_fusion.3), channel_id=1, source_target_pairs={{0,8},{8,16},{16,24},{24,32},{32,40},{40,48},{48,56},{56,64},{64,7... | collective-permute-start | bytes 1572872 | tf_op jit(solution)/shard_map/while/body/eval_jaxpr/ppermute | solution.py:18
  183.6 15.3 %collective-permute-start = (bf16[2,512,1,128]{3,1,2,0:T(8,128)(2,1)S(1)}, bf16[2,512,1,128]{3,1,2,0:T(8,128)(2,1)S(1)}, u32[]{:S(2)}, u32[]{:S(2)}) collective-permute-start(bf16[2,512,1,128]{3,1,2,0:T(8,128)(2,1)S(1)} %copy.51), channel_id=1, source_target_pairs={{0,8},{8,16},{16,24},{24,32},{32,40},{40,48},{48,56},{56,64},{64,7... | collective-permute-start | bytes 786440 | tf_op jit(solution)/shard_map/while/body/eval_jaxpr/ppermute | solution.py:18
  203.0 15.4 %collective-permute-start.1 = (f32[2,512,1,128]{3,1,2,0:T(8,128)S(1)}, f32[2,512,1,128]{3,1,2,0:T(8,128)S(1)}, u32[]{:S(2)}, u32[]{:S(2)}) collective-permute-start(f32[2,512,1,128]{3,1,2,0:T(8,128)S(1)} %convert_add_fusion.3), channel_id=1, source_target_pairs={{0,8},{8,16},{16,24},{24,32},{32,40},{40,48},{48,56},{56,64},{64,7... | collective-permute-start | bytes 1572872 | tf_op jit(solution)/shard_map/while/body/eval_jaxpr/ppermute | solution.py:18
  203.0 15.3 %collective-permute-start = (bf16[2,512,1,128]{3,1,2,0:T(8,128)(2,1)S(1)}, bf16[2,512,1,128]{3,1,2,0:T(8,128)(2,1)S(1)}, u32[]{:S(2)}, u32[]{:S(2)}) collective-permute-start(bf16[2,512,1,128]{3,1,2,0:T(8,128)(2,1)S(1)} %copy.51), channel_id=1, source_target_pairs={{0,8},{8,16},{16,24},{24,32},{32,40},{40,48},{48,56},{56,64},{64,7... | collective-permute-start | bytes 786440 | tf_op jit(solution)/shard_map/while/body/eval_jaxpr/ppermute | solution.py:18
  222.4 15.4 %collective-permute-start.1 = (f32[2,512,1,128]{3,1,2,0:T(8,128)S(1)}, f32[2,512,1,128]{3,1,2,0:T(8,128)S(1)}, u32[]{:S(2)}, u32[]{:S(2)}) collective-permute-start(f32[2,512,1,128]{3,1,2,0:T(8,128)S(1)} %convert_add_fusion.3), channel_id=1, source_target_pairs={{0,8},{8,16},{16,24},{24,32},{32,40},{40,48},{48,56},{56,64},{64,7... | collective-permute-start | bytes 1572872 | tf_op jit(solution)/shard_map/while/body/eval_jaxpr/ppermute | solution.py:18
  222.5 15.3 %collective-permute-start = (bf16[2,512,1,128]{3,1,2,0:T(8,128)(2,1)S(1)}, bf16[2,512,1,128]{3,1,2,0:T(8,128)(2,1)S(1)}, u32[]{:S(2)}, u32[]{:S(2)}) collective-permute-start(bf16[2,512,1,128]{3,1,2,0:T(8,128)(2,1)S(1)} %copy.51), channel_id=1, source_target_pairs={{0,8},{8,16},{16,24},{24,32},{32,40},{40,48},{48,56},{56,64},{64,7... | collective-permute-start | bytes 786440 | tf_op jit(solution)/shard_map/while/body/eval_jaxpr/ppermute | solution.py:18
  241.9 15.4 %collective-permute-start.1 = (f32[2,512,1,128]{3,1,2,0:T(8,128)S(1)}, f32[2,512,1,128]{3,1,2,0:T(8,128)S(1)}, u32[]{:S(2)}, u32[]{:S(2)}) collective-permute-start(f32[2,512,1,128]{3,1,2,0:T(8,128)S(1)} %convert_add_fusion.3), channel_id=1, source_target_pairs={{0,8},{8,16},{16,24},{24,32},{32,40},{40,48},{48,56},{56,64},{64,7... | collective-permute-start | bytes 1572872 | tf_op jit(solution)/shard_map/while/body/eval_jaxpr/ppermute | solution.py:18
  242.0 15.3 %collective-permute-start = (bf16[2,512,1,128]{3,1,2,0:T(8,128)(2,1)S(1)}, bf16[2,512,1,128]{3,1,2,0:T(8,128)(2,1)S(1)}, u32[]{:S(2)}, u32[]{:S(2)}) collective-permute-start(bf16[2,512,1,128]{3,1,2,0:T(8,128)(2,1)S(1)} %copy.51), channel_id=1, source_target_pairs={{0,8},{8,16},{16,24},{24,32},{32,40},{40,48},{48,56},{56,64},{64,7... | collective-permute-start | bytes 786440 | tf_op jit(solution)/shard_map/while/body/eval_jaxpr/ppermute | solution.py:18
  261.4 15.4 %collective-permute-start.1 = (f32[2,512,1,128]{3,1,2,0:T(8,128)S(1)}, f32[2,512,1,128]{3,1,2,0:T(8,128)S(1)}, u32[]{:S(2)}, u32[]{:S(2)}) collective-permute-start(f32[2,512,1,128]{3,1,2,0:T(8,128)S(1)} %convert_add_fusion.3), channel_id=1, source_target_pairs={{0,8},{8,16},{16,24},{24,32},{32,40},{40,48},{48,56},{56,64},{64,7... | collective-permute-start | bytes 1572872 | tf_op jit(solution)/shard_map/while/body/eval_jaxpr/ppermute | solution.py:18
  261.5 15.3 %collective-permute-start = (bf16[2,512,1,128]{3,1,2,0:T(8,128)(2,1)S(1)}, bf16[2,512,1,128]{3,1,2,0:T(8,128)(2,1)S(1)}, u32[]{:S(2)}, u32[]{:S(2)}) collective-permute-start(bf16[2,512,1,128]{3,1,2,0:T(8,128)(2,1)S(1)} %copy.51), channel_id=1, source_target_pairs={{0,8},{8,16},{16,24},{24,32},{32,40},{40,48},{48,56},{56,64},{64,7... | collective-permute-start | bytes 786440 | tf_op jit(solution)/shard_map/while/body/eval_jaxpr/ppermute | solution.py:18
  280.9 15.4 %collective-permute-start.1 = (f32[2,512,1,128]{3,1,2,0:T(8,128)S(1)}, f32[2,512,1,128]{3,1,2,0:T(8,128)S(1)}, u32[]{:S(2)}, u32[]{:S(2)}) collective-permute-start(f32[2,512,1,128]{3,1,2,0:T(8,128)S(1)} %convert_add_fusion.3), channel_id=1, source_target_pairs={{0,8},{8,16},{16,24},{24,32},{32,40},{40,48},{48,56},{56,64},{64,7... | collective-permute-start | bytes 1572872 | tf_op jit(solution)/shard_map/while/body/eval_jaxpr/ppermute | solution.py:18
  281.0 15.3 %collective-permute-start = (bf16[2,512,1,128]{3,1,2,0:T(8,128)(2,1)S(1)}, bf16[2,512,1,128]{3,1,2,0:T(8,128)(2,1)S(1)}, u32[]{:S(2)}, u32[]{:S(2)}) collective-permute-start(bf16[2,512,1,128]{3,1,2,0:T(8,128)(2,1)S(1)} %copy.51), channel_id=1, source_target_pairs={{0,8},{8,16},{16,24},{24,32},{32,40},{40,48},{48,56},{56,64},{64,7... | collective-permute-start | bytes 786440 | tf_op jit(solution)/shard_map/while/body/eval_jaxpr/ppermute | solution.py:18
  300.4 15.4 %collective-permute-start.1 = (f32[2,512,1,128]{3,1,2,0:T(8,128)S(1)}, f32[2,512,1,128]{3,1,2,0:T(8,128)S(1)}, u32[]{:S(2)}, u32[]{:S(2)}) collective-permute-start(f32[2,512,1,128]{3,1,2,0:T(8,128)S(1)} %convert_add_fusion.3), channel_id=1, source_target_pairs={{0,8},{8,16},{16,24},{24,32},{32,40},{40,48},{48,56},{56,64},{64,7... | collective-permute-start | bytes 1572872 | tf_op jit(solution)/shard_map/while/body/eval_jaxpr/ppermute | solution.py:18
  300.5 15.3 %collective-permute-start = (bf16[2,512,1,128]{3,1,2,0:T(8,128)(2,1)S(1)}, bf16[2,512,1,128]{3,1,2,0:T(8,128)(2,1)S(1)}, u32[]{:S(2)}, u32[]{:S(2)}) collective-permute-start(bf16[2,512,1,128]{3,1,2,0:T(8,128)(2,1)S(1)} %copy.51), channel_id=1, source_target_pairs={{0,8},{8,16},{16,24},{24,32},{32,40},{40,48},{48,56},{56,64},{64,7... | collective-permute-start | bytes 786440 | tf_op jit(solution)/shard_map/while/body/eval_jaxpr/ppermute | solution.py:18
  319.9 15.4 %collective-permute-start.1 = (f32[2,512,1,128]{3,1,2,0:T(8,128)S(1)}, f32[2,512,1,128]{3,1,2,0:T(8,128)S(1)}, u32[]{:S(2)}, u32[]{:S(2)}) collective-permute-start(f32[2,512,1,128]{3,1,2,0:T(8,128)S(1)} %convert_add_fusion.3), channel_id=1, source_target_pairs={{0,8},{8,16},{16,24},{24,32},{32,40},{40,48},{48,56},{56,64},{64,7... | collective-permute-start | bytes 1572872 | tf_op jit(solution)/shard_map/while/body/eval_jaxpr/ppermute | solution.py:18
  319.9 15.3 %collective-permute-start = (bf16[2,512,1,128]{3,1,2,0:T(8,128)(2,1)S(1)}, bf16[2,512,1,128]{3,1,2,0:T(8,128)(2,1)S(1)}, u32[]{:S(2)}, u32[]{:S(2)}) collective-permute-start(bf16[2,512,1,128]{3,1,2,0:T(8,128)(2,1)S(1)} %copy.51), channel_id=1, source_target_pairs={{0,8},{8,16},{16,24},{24,32},{32,40},{40,48},{48,56},{56,64},{64,7... | collective-permute-start | bytes 786440 | tf_op jit(solution)/shard_map/while/body/eval_jaxpr/ppermute | solution.py:18
  339.3 15.4 %collective-permute-start.1 = (f32[2,512,1,128]{3,1,2,0:T(8,128)S(1)}, f32[2,512,1,128]{3,1,2,0:T(8,128)S(1)}, u32[]{:S(2)}, u32[]{:S(2)}) collective-permute-start(f32[2,512,1,128]{3,1,2,0:T(8,128)S(1)} %convert_add_fusion.3), channel_id=1, source_target_pairs={{0,8},{8,16},{16,24},{24,32},{32,40},{40,48},{48,56},{56,64},{64,7... | collective-permute-start | bytes 1572872 | tf_op jit(solution)/shard_map/while/body/eval_jaxpr/ppermute | solution.py:18
  358.8 15.4 %collective-permute-start.1 = (f32[2,512,1,128]{3,1,2,0:T(8,128)S(1)}, f32[2,512,1,128]{3,1,2,0:T(8,128)S(1)}, u32[]{:S(2)}, u32[]{:S(2)}) collective-permute-start(f32[2,512,1,128]{3,1,2,0:T(8,128)S(1)} %convert_add_fusion.3), channel_id=1, source_target_pairs={{0,8},{8,16},{16,24},{24,32},{32,40},{40,48},{48,56},{56,64},{64,7... | collective-permute-start | bytes 1572872 | tf_op jit(solution)/shard_map/while/body/eval_jaxpr/ppermute | solution.py:18
  358.9 15.3 %collective-permute-start = (bf16[2,512,1,128]{3,1,2,0:T(8,128)(2,1)S(1)}, bf16[2,512,1,128]{3,1,2,0:T(8,128)(2,1)S(1)}, u32[]{:S(2)}, u32[]{:S(2)}) collective-permute-start(bf16[2,512,1,128]{3,1,2,0:T(8,128)(2,1)S(1)} %copy.51), channel_id=1, source_target_pairs={{0,8},{8,16},{16,24},{24,32},{32,40},{40,48},{48,56},{56,64},{64,7... | collective-permute-start | bytes 786440 | tf_op jit(solution)/shard_map/while/body/eval_jaxpr/ppermute | solution.py:18
  378.3 15.4 %collective-permute-start.1 = (f32[2,512,1,128]{3,1,2,0:T(8,128)S(1)}, f32[2,512,1,128]{3,1,2,0:T(8,128)S(1)}, u32[]{:S(2)}, u32[]{:S(2)}) collective-permute-start(f32[2,512,1,128]{3,1,2,0:T(8,128)S(1)} %convert_add_fusion.3), channel_id=1, source_target_pairs={{0,8},{8,16},{16,24},{24,32},{32,40},{40,48},{48,56},{56,64},{64,7... | collective-permute-start | bytes 1572872 | tf_op jit(solution)/shard_map/while/body/eval_jaxpr/ppermute | solution.py:18
  397.8 15.4 %collective-permute-start.1 = (f32[2,512,1,128]{3,1,2,0:T(8,128)S(1)}, f32[2,512,1,128]{3,1,2,0:T(8,128)S(1)}, u32[]{:S(2)}, u32[]{:S(2)}) collective-permute-start(f32[2,512,1,128]{3,1,2,0:T(8,128)S(1)} %convert_add_fusion.3), channel_id=1, source_target_pairs={{0,8},{8,16},{16,24},{24,32},{32,40},{40,48},{48,56},{56,64},{64,7... | collective-permute-start | bytes 1572872 | tf_op jit(solution)/shard_map/while/body/eval_jaxpr/ppermute | solution.py:18
  397.9 15.3 %collective-permute-start = (bf16[2,512,1,128]{3,1,2,0:T(8,128)(2,1)S(1)}, bf16[2,512,1,128]{3,1,2,0:T(8,128)(2,1)S(1)}, u32[]{:S(2)}, u32[]{:S(2)}) collective-permute-start(bf16[2,512,1,128]{3,1,2,0:T(8,128)(2,1)S(1)} %copy.51), channel_id=1, source_target_pairs={{0,8},{8,16},{16,24},{24,32},{32,40},{40,48},{48,56},{56,64},{64,7... | collective-permute-start | bytes 786440 | tf_op jit(solution)/shard_map/while/body/eval_jaxpr/ppermute | solution.py:18
  417.3 15.4 %collective-permute-start.1 = (f32[2,512,1,128]{3,1,2,0:T(8,128)S(1)}, f32[2,512,1,128]{3,1,2,0:T(8,128)S(1)}, u32[]{:S(2)}, u32[]{:S(2)}) collective-permute-start(f32[2,512,1,128]{3,1,2,0:T(8,128)S(1)} %convert_add_fusion.3), channel_id=1, source_target_pairs={{0,8},{8,16},{16,24},{24,32},{32,40},{40,48},{48,56},{56,64},{64,7... | collective-permute-start | bytes 1572872 | tf_op jit(solution)/shard_map/while/body/eval_jaxpr/ppermute | solution.py:18
  436.7 15.4 %collective-permute-start.1 = (f32[2,512,1,128]{3,1,2,0:T(8,128)S(1)}, f32[2,512,1,128]{3,1,2,0:T(8,128)S(1)}, u32[]{:S(2)}, u32[]{:S(2)}) collective-permute-start(f32[2,512,1,128]{3,1,2,0:T(8,128)S(1)} %convert_add_fusion.3), channel_id=1, source_target_pairs={{0,8},{8,16},{16,24},{24,32},{32,40},{40,48},{48,56},{56,64},{64,7... | collective-permute-start | bytes 1572872 | tf_op jit(solution)/shard_map/while/body/eval_jaxpr/ppermute | solution.py:18
  436.8 15.3 %collective-permute-start = (bf16[2,512,1,128]{3,1,2,0:T(8,128)(2,1)S(1)}, bf16[2,512,1,128]{3,1,2,0:T(8,128)(2,1)S(1)}, u32[]{:S(2)}, u32[]{:S(2)}) collective-permute-start(bf16[2,512,1,128]{3,1,2,0:T(8,128)(2,1)S(1)} %copy.51), channel_id=1, source_target_pairs={{0,8},{8,16},{16,24},{24,32},{32,40},{40,48},{48,56},{56,64},{64,7... | collective-permute-start | bytes 786440 | tf_op jit(solution)/shard_map/while/body/eval_jaxpr/ppermute | solution.py:18
  456.2 15.4 %collective-permute-start.1 = (f32[2,512,1,128]{3,1,2,0:T(8,128)S(1)}, f32[2,512,1,128]{3,1,2,0:T(8,128)S(1)}, u32[]{:S(2)}, u32[]{:S(2)}) collective-permute-start(f32[2,512,1,128]{3,1,2,0:T(8,128)S(1)} %convert_add_fusion.3), channel_id=1, source_target_pairs={{0,8},{8,16},{16,24},{24,32},{32,40},{40,48},{48,56},{56,64},{64,7... | collective-permute-start | bytes 1572872 | tf_op jit(solution)/shard_map/while/body/eval_jaxpr/ppermute | solution.py:18
  475.7 15.4 %collective-permute-start.1 = (f32[2,512,1,128]{3,1,2,0:T(8,128)S(1)}, f32[2,512,1,128]{3,1,2,0:T(8,128)S(1)}, u32[]{:S(2)}, u32[]{:S(2)}) collective-permute-start(f32[2,512,1,128]{3,1,2,0:T(8,128)S(1)} %convert_add_fusion.3), channel_id=1, source_target_pairs={{0,8},{8,16},{16,24},{24,32},{32,40},{40,48},{48,56},{56,64},{64,7... | collective-permute-start | bytes 1572872 | tf_op jit(solution)/shard_map/while/body/eval_jaxpr/ppermute | solution.py:18
  475.8 15.3 %collective-permute-start = (bf16[2,512,1,128]{3,1,2,0:T(8,128)(2,1)S(1)}, bf16[2,512,1,128]{3,1,2,0:T(8,128)(2,1)S(1)}, u32[]{:S(2)}, u32[]{:S(2)}) collective-permute-start(bf16[2,512,1,128]{3,1,2,0:T(8,128)(2,1)S(1)} %copy.51), channel_id=1, source_target_pairs={{0,8},{8,16},{16,24},{24,32},{32,40},{40,48},{48,56},{56,64},{64,7... | collective-permute-start | bytes 786440 | tf_op jit(solution)/shard_map/while/body/eval_jaxpr/ppermute | solution.py:18
  495.2 15.4 %collective-permute-start.1 = (f32[2,512,1,128]{3,1,2,0:T(8,128)S(1)}, f32[2,512,1,128]{3,1,2,0:T(8,128)S(1)}, u32[]{:S(2)}, u32[]{:S(2)}) collective-permute-start(f32[2,512,1,128]{3,1,2,0:T(8,128)S(1)} %convert_add_fusion.3), channel_id=1, source_target_pairs={{0,8},{8,16},{16,24},{24,32},{32,40},{40,48},{48,56},{56,64},{64,7... | collective-permute-start | bytes 1572872 | tf_op jit(solution)/shard_map/while/body/eval_jaxpr/ppermute | solution.py:18
  514.7 15.4 %collective-permute-start.1 = (f32[2,512,1,128]{3,1,2,0:T(8,128)S(1)}, f32[2,512,1,128]{3,1,2,0:T(8,128)S(1)}, u32[]{:S(2)}, u32[]{:S(2)}) collective-permute-start(f32[2,512,1,128]{3,1,2,0:T(8,128)S(1)} %convert_add_fusion.3), channel_id=1, source_target_pairs={{0,8},{8,16},{16,24},{24,32},{32,40},{40,48},{48,56},{56,64},{64,7... | collective-permute-start | bytes 1572872 | tf_op jit(solution)/shard_map/while/body/eval_jaxpr/ppermute | solution.py:18
  514.8 15.3 %collective-permute-start = (bf16[2,512,1,128]{3,1,2,0:T(8,128)(2,1)S(1)}, bf16[2,512,1,128]{3,1,2,0:T(8,128)(2,1)S(1)}, u32[]{:S(2)}, u32[]{:S(2)}) collective-permute-start(bf16[2,512,1,128]{3,1,2,0:T(8,128)(2,1)S(1)} %copy.51), channel_id=1, source_target_pairs={{0,8},{8,16},{16,24},{24,32},{32,40},{40,48},{48,56},{56,64},{64,7... | collective-permute-start | bytes 786440 | tf_op jit(solution)/shard_map/while/body/eval_jaxpr/ppermute | solution.py:18
  534.2 15.4 %collective-permute-start.1 = (f32[2,512,1,128]{3,1,2,0:T(8,128)S(1)}, f32[2,512,1,128]{3,1,2,0:T(8,128)S(1)}, u32[]{:S(2)}, u32[]{:S(2)}) collective-permute-start(f32[2,512,1,128]{3,1,2,0:T(8,128)S(1)} %convert_add_fusion.3), channel_id=1, source_target_pairs={{0,8},{8,16},{16,24},{24,32},{32,40},{40,48},{48,56},{56,64},{64,7... | collective-permute-start | bytes 1572872 | tf_op jit(solution)/shard_map/while/body/eval_jaxpr/ppermute | solution.py:18
  534.2 15.3 %collective-permute-start = (bf16[2,512,1,128]{3,1,2,0:T(8,128)(2,1)S(1)}, bf16[2,512,1,128]{3,1,2,0:T(8,128)(2,1)S(1)}, u32[]{:S(2)}, u32[]{:S(2)}) collective-permute-start(bf16[2,512,1,128]{3,1,2,0:T(8,128)(2,1)S(1)} %copy.51), channel_id=1, source_target_pairs={{0,8},{8,16},{16,24},{24,32},{32,40},{40,48},{48,56},{56,64},{64,7... | collective-permute-start | bytes 786440 | tf_op jit(solution)/shard_map/while/body/eval_jaxpr/ppermute | solution.py:18
  553.6 15.4 %collective-permute-start.1 = (f32[2,512,1,128]{3,1,2,0:T(8,128)S(1)}, f32[2,512,1,128]{3,1,2,0:T(8,128)S(1)}, u32[]{:S(2)}, u32[]{:S(2)}) collective-permute-start(f32[2,512,1,128]{3,1,2,0:T(8,128)S(1)} %convert_add_fusion.3), channel_id=1, source_target_pairs={{0,8},{8,16},{16,24},{24,32},{32,40},{40,48},{48,56},{56,64},{64,7... | collective-permute-start | bytes 1572872 | tf_op jit(solution)/shard_map/while/body/eval_jaxpr/ppermute | solution.py:18
  553.7 15.3 %collective-permute-start = (bf16[2,512,1,128]{3,1,2,0:T(8,128)(2,1)S(1)}, bf16[2,512,1,128]{3,1,2,0:T(8,128)(2,1)S(1)}, u32[]{:S(2)}, u32[]{:S(2)}) collective-permute-start(bf16[2,512,1,128]{3,1,2,0:T(8,128)(2,1)S(1)} %copy.51), channel_id=1, source_target_pairs={{0,8},{8,16},{16,24},{24,32},{32,40},{40,48},{48,56},{56,64},{64,7... | collective-permute-start | bytes 786440 | tf_op jit(solution)/shard_map/while/body/eval_jaxpr/ppermute | solution.py:18
  573.1 15.4 %collective-permute-start.1 = (f32[2,512,1,128]{3,1,2,0:T(8,128)S(1)}, f32[2,512,1,128]{3,1,2,0:T(8,128)S(1)}, u32[]{:S(2)}, u32[]{:S(2)}) collective-permute-start(f32[2,512,1,128]{3,1,2,0:T(8,128)S(1)} %convert_add_fusion.3), channel_id=1, source_target_pairs={{0,8},{8,16},{16,24},{24,32},{32,40},{40,48},{48,56},{56,64},{64,7... | collective-permute-start | bytes 1572872 | tf_op jit(solution)/shard_map/while/body/eval_jaxpr/ppermute | solution.py:18
  592.6 15.4 %collective-permute-start.1 = (f32[2,512,1,128]{3,1,2,0:T(8,128)S(1)}, f32[2,512,1,128]{3,1,2,0:T(8,128)S(1)}, u32[]{:S(2)}, u32[]{:S(2)}) collective-permute-start(f32[2,512,1,128]{3,1,2,0:T(8,128)S(1)} %convert_add_fusion.3), channel_id=1, source_target_pairs={{0,8},{8,16},{16,24},{24,32},{32,40},{40,48},{48,56},{56,64},{64,7... | collective-permute-start | bytes 1572872 | tf_op jit(solution)/shard_map/while/body/eval_jaxpr/ppermute | solution.py:18
  592.7 15.3 %collective-permute-start = (bf16[2,512,1,128]{3,1,2,0:T(8,128)(2,1)S(1)}, bf16[2,512,1,128]{3,1,2,0:T(8,128)(2,1)S(1)}, u32[]{:S(2)}, u32[]{:S(2)}) collective-permute-start(bf16[2,512,1,128]{3,1,2,0:T(8,128)(2,1)S(1)} %copy.51), channel_id=1, source_target_pairs={{0,8},{8,16},{16,24},{24,32},{32,40},{40,48},{48,56},{56,64},{64,7... | collective-permute-start | bytes 786440 | tf_op jit(solution)/shard_map/while/body/eval_jaxpr/ppermute | solution.py:18
  612.1 15.4 %collective-permute-start.1 = (f32[2,512,1,128]{3,1,2,0:T(8,128)S(1)}, f32[2,512,1,128]{3,1,2,0:T(8,128)S(1)}, u32[]{:S(2)}, u32[]{:S(2)}) collective-permute-start(f32[2,512,1,128]{3,1,2,0:T(8,128)S(1)} %convert_add_fusion.3), channel_id=1, source_target_pairs={{0,8},{8,16},{16,24},{24,32},{32,40},{40,48},{48,56},{56,64},{64,7... | collective-permute-start | bytes 1572872 | tf_op jit(solution)/shard_map/while/body/eval_jaxpr/ppermute | solution.py:18
  612.2 15.3 %collective-permute-start = (bf16[2,512,1,128]{3,1,2,0:T(8,128)(2,1)S(1)}, bf16[2,512,1,128]{3,1,2,0:T(8,128)(2,1)S(1)}, u32[]{:S(2)}, u32[]{:S(2)}) collective-permute-start(bf16[2,512,1,128]{3,1,2,0:T(8,128)(2,1)S(1)} %copy.51), channel_id=1, source_target_pairs={{0,8},{8,16},{16,24},{24,32},{32,40},{40,48},{48,56},{56,64},{64,7... | collective-permute-start | bytes 786440 | tf_op jit(solution)/shard_map/while/body/eval_jaxpr/ppermute | solution.py:18
  (29 other events, 1017.7 us)
Sparse Core Ops, SparseCore 0:
  641.2 111.8 reduce-scatter.1
